TPU v7x, 128 devices: a whole 4x4x4 slice. The times are simulated.
128 devices in a mesh: segment: 4 (over x), dp: 32 (over y, z, core).
Axes of the slice: x: 4, y: 4, z: 4, core: 2. Of those that a mesh axis runs over, the one named last changes fastest.
Arguments:
- query_states: bfloat16 [1024, 32, 768], P('dp'), may hold values from -40 to 40
- passage_states: bfloat16 [512, 64, 768], P('dp'), may hold values from -40 to 40
- query_tokens: int32 [1024, 32], P('dp'), may hold values from 0 to 32099, as said below
- passage_tokens: int32 [512, 64], P('dp'), may hold values from 0 to 32099, as said below
- ff_gains: float32 [2, 768], replicated, may hold values from 0.1 to 1.9
- out_gains: float32 [2, 768], replicated, may hold values from 0.1 to 1.9
- w_gate: bfloat16 [2, 768, 2048], P(None, None, 'segment'), may hold values from -0.21875 to 0.21875
- w_up: bfloat16 [2, 768, 2048], P(None, None, 'segment'), may hold values from -0.21875 to 0.21875
- w_down: bfloat16 [2, 2048, 768], P(None, 'segment'), may hold values from -1 to 1
- w_proj: bfloat16 [2, 768, 768], replicated, may hold values from -0.21875 to 0.21875
- positive_ids: int32 [1024], P('dp'), may hold values from 0 to 511
- negative_ids: int32 [1024, 15], P('dp'), may hold values from 0 to 511
- negative_counts: int32 [1024], P('dp'), may hold values from 1 to 15, 7680 in all
Outputs:
- grad_gate: float32 [2, 768, 2048], P(None, 'dp', 'segment')
- grad_up: float32 [2, 768, 2048], P(None, 'dp', 'segment')
- grad_down: float32 [2, 2048, 768], P(None, 'segment', 'dp')
Inputs may be any that keep to these rules, and one draw needn't show every extreme that they name: `query_tokens`: each row holds token ids of 1 or more followed by zeros, at least 8 nonzero ids; the first row has no zeros. `passage_tokens`: each row holds token ids of 1 or more followed by zeros, at least 16 nonzero ids; the first row has no zeros. Only the first negative_counts[i] entries of row i are used; the counts sum to 7680.
All inputs are finite; a program needn't handle non-finite values. No bound on the sum of `negative_counts` on one device may be relied on, other than what follows from the above.
Results may differ from a plain program's by a relative error of at most 0.012.
Values may be sent and summed in bfloat16 or wider, within the bound.
No kernel may reach another device: no remote copies, remote signals or barrier semaphores. Data moves between devices by JAX's collectives and lax.ppermute only.
A program may use at most 128 MiB of HBM per device.

v0:
```python
import jax
import jax.numpy as jnp
from jax import lax
from jax.sharding import PartitionSpec as P

score_temp = 0.05
rank_temp = 1.0
recall_depth = 5.0
loss_scale = 16.0
norm_eps = 1e-06


def inverse_rms(values):
    return lax.rsqrt(jnp.mean(values * values, axis=-1, keepdims=True) + norm_eps)


def normed_input(states, ff_gain):
    widened = states.astype(jnp.float32)
    return (widened * inverse_rms(widened) * ff_gain).astype(jnp.bfloat16)


def pooled_embedding(summed, tokens, out_gain, proj_weight):
    normed = summed * inverse_rms(summed) * out_gain
    token_mask = (tokens != 0).astype(jnp.float32)[:, :, None]
    pooled = jnp.sum(normed * token_mask, axis=1) / jnp.sum(token_mask, axis=1)
    projected = jnp.dot(pooled, proj_weight.astype(jnp.float32), precision=lax.Precision.HIGHEST)
    return projected * lax.rsqrt(jnp.sum(projected * projected, axis=-1, keepdims=True) + norm_eps)


def recall_loss(scores, valid_mask):
    margins = (scores[:, 1:] - scores[:, :1]) / score_temp
    soft_ranks = 1.0 + jnp.sum(jax.nn.sigmoid(margins) * valid_mask, axis=1)
    return loss_scale * jnp.sum(jax.nn.sigmoid((soft_ranks - recall_depth - 0.5) / rank_temp))


def contract(left, right):
    return lax.dot_general(
        left, right, (((0,), (0,)), ((), ())), preferred_element_type=jnp.float32
    )


def natural_order(gathered, segments, groups, per_device):
    model_width = gathered.shape[-1]
    shaped = gathered.reshape(segments, groups, per_device, model_width)
    return jnp.transpose(shaped, (1, 0, 2, 3)).reshape(-1, model_width)


def score_grads_of(scores, counts):
    slots = scores.shape[1] - 1
    valid_mask = (
        lax.broadcasted_iota(jnp.int32, (scores.shape[0], slots), 1) < counts[:, None]
    ).astype(jnp.float32)
    return jax.grad(recall_loss)(scores, valid_mask)


def body(
    query_states,
    passage_states,
    query_tokens,
    passage_tokens,
    ff_gains,
    out_gains,
    w_gate,
    w_up,
    w_down,
    w_proj,
    positive_ids,
    negative_ids,
    negative_counts,
):
    segments = lax.axis_size("segment")
    groups = lax.axis_size("dp")
    segment_index = lax.axis_index("segment")
    model_width = query_states.shape[-1]
    query_dev = query_states.shape[0] // segments
    passage_dev = passage_states.shape[0] // segments

    def forward_part(states, tower_index):
        normed = normed_input(states, ff_gains[tower_index]).reshape(-1, model_width)
        gate_pre = jnp.dot(normed, w_gate[tower_index], preferred_element_type=jnp.float32)
        up_pre = jnp.dot(normed, w_up[tower_index], preferred_element_type=jnp.float32)
        activated, gelu_back = jax.vjp(jax.nn.gelu, gate_pre)
        hidden = (activated * up_pre).astype(jnp.bfloat16)
        branch = jnp.dot(hidden, w_down[tower_index], preferred_element_type=jnp.float32).reshape(
            states.shape
        )
        return (normed, up_pre, activated, gelu_back, hidden, branch)

    def own_rows(values, per_device):
        return lax.dynamic_slice_in_dim(values, segment_index * per_device, per_device, 0)

    def head_of(tokens, tower_index):
        return lambda summed: pooled_embedding(
            summed, tokens, out_gains[tower_index], w_proj[tower_index]
        )

    query_parts = forward_part(query_states, 0)
    passage_parts = forward_part(passage_states, 1)
    query_branch, passage_branch = (
        lax.psum_scatter(query_parts[5], "segment", scatter_dimension=0, tiled=True),
        lax.psum_scatter(passage_parts[5], "segment", scatter_dimension=0, tiled=True),
    )
    query_embed, query_back = jax.vjp(
        head_of(own_rows(query_tokens, query_dev), 0),
        own_rows(query_states, query_dev).astype(jnp.float32) + query_branch,
    )
    passage_embed, passage_back = jax.vjp(
        head_of(own_rows(passage_tokens, passage_dev), 1),
        own_rows(passage_states, passage_dev).astype(jnp.float32) + passage_branch,
    )
    query_round = query_embed.astype(jnp.bfloat16)
    passage_round = passage_embed.astype(jnp.bfloat16)
    passage_mixed = lax.all_gather(passage_round, ("segment", "dp"), axis=0, tiled=True)
    passage_all = natural_order(passage_mixed, segments, groups, passage_dev)
    cand_ids = jnp.concatenate(
        [own_rows(positive_ids, query_dev)[:, None], own_rows(negative_ids, query_dev)], axis=1
    )
    cand_rows = passage_all[cand_ids]
    scores = jnp.einsum("qd,qcd->qc", query_round, cand_rows, preferred_element_type=jnp.float32)
    score_grads = score_grads_of(scores, own_rows(negative_counts, query_dev))
    query_grad = jnp.einsum(
        "qc,qcd->qd", score_grads, cand_rows.astype(jnp.float32), precision=lax.Precision.HIGHEST
    )
    passage_total = passage_all.shape[0]
    every_id = lax.broadcasted_iota(jnp.int32, (1, 1, passage_total), 2)
    matches = (cand_ids[:, :, None] == every_id).astype(jnp.float32)
    coefficient = jnp.einsum("qcp,qc->pq", matches, score_grads, precision=lax.Precision.HIGHEST)
    natural_grads = jnp.dot(
        coefficient, query_round.astype(jnp.float32), precision=lax.Precision.HIGHEST
    )
    mixed_grads = jnp.transpose(
        natural_grads.reshape(groups, segments, passage_dev, model_width), (1, 0, 2, 3)
    ).reshape(passage_total, model_width)
    passage_grad = lax.psum_scatter(mixed_grads, ("segment", "dp"), scatter_dimension=0, tiled=True)
    query_share = query_back(query_grad)[0].astype(jnp.bfloat16)
    passage_share = passage_back(passage_grad)[0].astype(jnp.bfloat16)
    query_rows, passage_rows = (
        lax.all_gather(query_share, "segment", axis=0, tiled=True),
        lax.all_gather(passage_share, "segment", axis=0, tiled=True),
    )

    def backward_part(tower_parts, row_grads, tower_index):
        normed, up_pre, activated, gelu_back, hidden, branch = tower_parts
        flat_grad = row_grads.reshape(-1, model_width)
        hidden_grad = lax.dot_general(
            flat_grad,
            w_down[tower_index],
            (((1,), (1,)), ((), ())),
            preferred_element_type=jnp.float32,
        )
        gate_grad = gelu_back(hidden_grad * up_pre)[0].astype(jnp.bfloat16)
        up_grad = (hidden_grad * activated).astype(jnp.bfloat16)
        return (normed, gate_grad, up_grad, hidden, flat_grad)

    towers_back = (
        backward_part(query_parts, query_rows, 0),
        backward_part(passage_parts, passage_rows, 1),
    )

    def weight_terms():
        matrices = [[], [], []]
        for normed, gate_grad, up_grad, hidden, flat_grad in towers_back:
            matrices[0].append(contract(normed, gate_grad))
            matrices[1].append(contract(normed, up_grad))
            matrices[2].append(contract(flat_grad, hidden))
        return jnp.stack([jnp.stack(pieces, axis=1) for pieces in matrices], axis=1)

    summed_grads = lax.psum_scatter(weight_terms(), "dp", scatter_dimension=0, tiled=True)
    grad_gate = jnp.transpose(summed_grads[:, 0], (1, 0, 2))
    grad_up = jnp.transpose(summed_grads[:, 1], (1, 0, 2))
    grad_down = jnp.transpose(summed_grads[:, 2], (1, 2, 0))
    return (grad_gate, grad_up, grad_down)


def solution(mesh):
    return jax.shard_map(
        body,
        mesh=mesh,
        in_specs=(
            P("dp", None, None),
            P("dp", None, None),
            P("dp", None),
            P("dp", None),
            P(),
            P(),
            P(None, None, "segment"),
            P(None, None, "segment"),
            P(None, "segment", None),
            P(),
            P("dp"),
            P("dp", None),
            P("dp"),
        ),
        out_specs=(P(None, "dp", "segment"), P(None, "dp", "segment"), P(None, "segment", "dp")),
        check_vma=False,
    )
```

profile of v0, /device:TPU:0, one launch (start us, length us, event | category | flops | bytes accessed | tf_op | source)
XLA Modules:
  0.0 478.4 jit_solution(3566909360010617595)
XLA Ops:
  7.2 0.8 slice_reduce_fusion.3
  8.1 1.9 fusion
  10.5 1.0 fusion.56
  11.6 0.8 copy-done.23
  12.5 2.6 multiply_convert_fusion.3
  15.0 1.0 copy-done.15
  16.0 2.6 fusion.50
  18.7 1.3 copy-done.3
  21.5 1.0 fusion.48
  22.9 2.6 multiply_convert_fusion.2
  25.5 1.0 copy-done.16
  26.6 2.7 fusion.42
  32.3 27.3 %reduce-scatter.4.cloned.1.call-done = f32[8,32,768]{2,1,0:T(8,128)} async-done(((f32[32,32,768]{2,1,0:T(8,128)}), f32[8,32,768]{2,1,0:T(8,128)}) %reduce-scatter.4.cloned.1.call-update) | async-done | bytes 786448 | tf_op jit(solution)/shard_map/reduce_scatter | solution.py:100
  59.6 1.5 multiply_reduce_fusion.5
  61.1 1.4 multiply_reduce_fusion.4
  63.3 36.7 %reduce-scatter.6.cloned.1.call-done = f32[4,64,768]{2,1,0:T(8,128)} async-done(((f32[16,64,768]{2,1,0:T(8,128)}), f32[4,64,768]{2,1,0:T(8,128)}) %reduce-scatter.6.cloned.1.call-update) | async-done | bytes 786448 | tf_op jit(solution)/shard_map/reduce_scatter | solution.py:101
  100.0 1.5 multiply_reduce_fusion.3
  101.5 1.4 multiply_reduce_fusion.2
  103.7 36.7 %all-gather = bf16[128,4,768]{2,1,0:T(4,128)(2,1)S(1)} all-gather(bf16[1,4,768]{2,1,0:T(4,128)(2,1)S(1)} %fusion.91), channel_id=1, replica_groups=mesh['segment'=4,'dp'=32] {'segment','dp'}, dimensions={0}, use_global_device_ids=true | all-gather | bytes 792576 | tf_op jit(solution)/shard_map/all_gather | solution.py:113
  140.4 1.1 copy.44
  141.5 2.3 reshape.216
  143.9 2.2 gather_fusion
  147.2 2.0 fusion.74
  149.1 2.7 reshape.218
  151.9 2.7 copy.25
  154.5 2.8 reshape.219
  157.4 2.4 fusion.28
  159.8 1.5 multiply_reduce_fusion.1
  161.2 1.0 fusion.40
  162.4 141.9 %all-reduce.5.cloned.1.call-done = f32[512,768]{1,0:T(8,128)} async-done(((f32[512,768]{1,0:T(8,128)}), f32[512,768]{1,0:T(8,128)}) %all-reduce.5.cloned.1.call-update) | async-done | bytes 1572880
  304.3 0.9 multiply_reduce_fusion.7
  305.2 2.4 fusion.31
  307.5 1.4 multiply_reduce_fusion
  309.0 1.1 fusion.41
  310.3 19.9 %all-gather.4.cloned.1.call-done = bf16[32,32,768]{2,1,0:T(8,128)(2,1)} async-done(((bf16[8,32,768]{2,1,0:T(8,128)(2,1)}), bf16[32,32,768]{2,1,0:T(8,128)(2,1)}) %all-gather.4.cloned.1.call-update) | async-done | bytes 1572880 | tf_op jit(solution)/shard_map/all_gather | solution.py:138
  330.3 4.0 convolution_bitcast_fusion.1
  334.3 1.0 fusion.52
  336.4 1.1 convolution_bitcast_fusion.3
  338.0 3.1 convolution_bitcast_fusion.5
  341.0 17.2 %all-gather.6.cloned.1.call-done = bf16[16,64,768]{2,1,0:T(8,128)(2,1)} async-done(((bf16[4,64,768]{2,1,0:T(8,128)(2,1)}), bf16[16,64,768]{2,1,0:T(8,128)(2,1)}) %all-gather.6.cloned.1.call-update) | async-done | bytes 1572880 | tf_op jit(solution)/shard_map/all_gather | solution.py:139
  358.2 2.8 convolution_bitcast_fusion
  361.1 1.0 fusion.44
  363.1 1.1 convolution_bitcast_fusion.2
  364.7 2.4 convolution_bitcast_fusion.4
  367.4 1.1 copy-done.9
  369.2 4.7 pad_maximum_fusion
  374.0 95.9 %reduce-scatter.8.cloned.1.call-done = f32[24,3,2,512]{3,0,2,1:T(8,128)} async-done(((f32[768,3,2,512]{3,0,2,1:T(8,128)}), f32[24,3,2,512]{3,0,2,1:T(8,128)}) %reduce-scatter.8.cloned.1.call-update) | async-done | bytes 294928 | tf_op jit(solution)/shard_map/reduce_scatter | solution.py:168
  469.9 1.7 slice_bitcast_fusion
  (119 shorter events, 12.7 us)
Async XLA Ops:
  7.2 23.1 %copy-start = (s32[32,15]{0,1:T(8,128)S(1)}, s32[32,15]{0,1:T(8,128)}, u32[]{:S(2)}) copy-start(s32[32,15]{0,1:T(8,128)} %param.24) | copy-start | bytes 5764
  7.2 2.8 copy-start.2
  7.2 52.4 %reduce-scatter.4.cloned.1.call-start = ((), (), s32[]{:S(2)}) async-start(), calls=%async_computation.3 | async-start | bytes 3932160 | tf_op jit(solution)/shard_map/reduce_scatter | solution.py:100
  8.1 2.4 copy-start.21
  10.5 1.2 copy-start.10
  10.5 2.0 copy-start.23
  12.4 2.6 copy-start.28
  12.5 3.6 copy-start.6
  15.0 1.0 copy-start.15
  18.7 1.4 copy-start.3
  18.7 81.3 %reduce-scatter.6.cloned.1.call-start = ((), (), s32[]{:S(2)}) async-start(), calls=%async_computation.4 | async-start | bytes 3932160 | tf_op jit(solution)/shard_map/reduce_scatter | solution.py:101
  20.1 1.4 copy-start.22
  20.9 1.6 copy-start.12
  21.5 1.4 copy-start.24
  22.9 2.6 copy-start.30
  22.9 3.7 copy-start.7
  25.5 1.0 copy-start.16
  29.2 0.7 copy-start.27
  29.2 0.7 copy-start.18
  29.3 3.0 copy-start.17
  29.3 275.0 %all-reduce.5.cloned.1.call-start = ((), (), s32[]{:S(2)}) async-start(), calls=%async_computation.8 | async-start | bytes 3145728
  59.6 2.9 copy-start.19
  100.0 2.9 copy-start.20
  157.3 173.0 %all-gather.4.cloned.1.call-start = ((), (), s32[]{:S(2)}) async-start(), calls=%async_computation.5 | async-start | bytes 1966080 | tf_op jit(solution)/shard_map/all_gather | solution.py:138
  157.4 3.9 copy-start.4
  162.3 146.7 %copy-start.5 = (f32[4,64,768]{2,1,0:T(8,128)S(1)}, f32[4,64,768]{2,1,0:T(8,128)}, u32[]{:S(2)}) copy-start(f32[4,64,768]{2,1,0:T(8,128)} %reduce-scatter.6.cloned.1.call-done) | copy-start | bytes 2359300
  162.3 195.9 %all-gather.6.cloned.1.call-start = ((), (), s32[]{:S(2)}) async-start(), calls=%async_computation.6 | async-start | bytes 1966080 | tf_op jit(solution)/shard_map/all_gather | solution.py:139
  310.1 159.8 %reduce-scatter.8.cloned.1.call-start = ((), (), s32[]{:S(2)}) async-start(), calls=%async_computation.7 | async-start | bytes 9732096 | tf_op jit(solution)/shard_map/reduce_scatter | solution.py:168
  330.3 4.0 copy-start.8
  330.3 4.0 copy-start.25
  334.3 1.4 copy-start.11
  334.3 2.1 copy-start.29
  336.4 1.6 copy-start.32
  358.2 2.8 copy-start.26
  361.1 1.4 copy-start.13
  361.1 2.1 copy-start.31
  363.1 1.6 copy-start.33
  364.7 2.4 copy-start.14
  367.1 1.4 copy-start.9
  374.0 97.6 %copy-start.1 = (s32[32,15]{0,1:T(8,128)S(1)}, s32[32,15]{0,1:T(8,128)}, u32[]{:S(2)}) copy-start(s32[32,15]{0,1:T(8,128)} %param.24) | copy-start | bytes 5764
Sparse Core Ops, SparseCore 0:
  18.8 40.7 reduce-scatter.3
  62.0 37.9 reduce-scatter.5
  157.4 146.8 all-reduce.4
  305.8 24.4 all-gather.3
  331.8 26.4 all-gather.5
  374.1 95.7 reduce-scatter.7
where the time goes:
time: 479 us; the launch traced here: 478 us
  waiting for transfers between devices  339 us (71%)
  matrix products  37.9 us (8%)
  blocking collectives  36.7 us (8%)
  local copies, waits for them, and re-layouts  27.1 us (6%)
  other arithmetic  22.7 us (5%)
  between operations  14.5 us (3%)
    unnamed x7, waiting for transfers between devices  142 us
    reduce_scatter x1, waiting for transfers between devices, body(): lax.psum_scatter(weight_terms(), 'dp', scatter_dimension=0, tiled=True)  95.9 us
    reduce_scatter x1, waiting for transfers between devices, body(): lax.psum_scatter(passage_parts[5], 'segment', scatter_dimension=0, tiled=...  36.7 us
    all_gather x1, blocking collectives, body(): lax.all_gather(passage_round, ('segment', 'dp'), axis=0, tiled=True)  36.7 us
    reduce_scatter x1, waiting for transfers between devices, body(): lax.psum_scatter(query_parts[5], 'segment', scatter_dimension=0, tiled=True)  27.3 us
    all_gather x1, waiting for transfers between devices, body(): lax.all_gather(query_share, 'segment', axis=0, tiled=True)  19.9 us
    all_gather x1, waiting for transfers between devices, body(): lax.all_gather(passage_share, 'segment', axis=0, tiled=True)  17.2 us
    dot_general x6, matrix products, contract(): lax.dot_general(left, right, (((0,), (0,)), ((), ())), preferred_element_...  14.5 us
  transfers between devices with their start and end apart: 6, of which 6 were waited for; matrix products, arithmetic and copies ran while one was open for 7% of the time, Pallas kernels for 0%

commit v1 on v0

--- a/solution.py
+++ b/solution.py
@@ -110,8 +110,8 @@
     )
     query_round = query_embed.astype(jnp.bfloat16)
     passage_round = passage_embed.astype(jnp.bfloat16)
-    passage_mixed = lax.all_gather(passage_round, ("segment", "dp"), axis=0, tiled=True)
-    passage_all = natural_order(passage_mixed, segments, groups, passage_dev)
+    passage_group = lax.all_gather(passage_round, "segment", axis=0, tiled=True)
+    passage_all = lax.all_gather(passage_group, "dp", axis=0, tiled=True)
     cand_ids = jnp.concatenate(
         [own_rows(positive_ids, query_dev)[:, None], own_rows(negative_ids, query_dev)], axis=1
     )
@@ -128,10 +128,8 @@
     natural_grads = jnp.dot(
         coefficient, query_round.astype(jnp.float32), precision=lax.Precision.HIGHEST
     )
-    mixed_grads = jnp.transpose(
-        natural_grads.reshape(groups, segments, passage_dev, model_width), (1, 0, 2, 3)
-    ).reshape(passage_total, model_width)
-    passage_grad = lax.psum_scatter(mixed_grads, ("segment", "dp"), scatter_dimension=0, tiled=True)
+    group_grads = lax.psum_scatter(natural_grads, "dp", scatter_dimension=0, tiled=True)
+    passage_grad = lax.psum_scatter(group_grads, "segment", scatter_dimension=0, tiled=True)
     query_share = query_back(query_grad)[0].astype(jnp.bfloat16)
     passage_share = passage_back(passage_grad)[0].astype(jnp.bfloat16)
     query_rows, passage_rows = (

time: 479 us -> 401 us (0.84)
  waiting for transfers between devices: 339 us -> 252 us
  blocking collectives: 36.7 us -> 57.6 us
  local copies, waits for them, and re-layouts: 27.1 us -> 15.1 us
    unnamed x7 -> x6, waiting for transfers between devices: 142 us -> 0.1 us
    reduce_scatter x0 -> x1, waiting for transfers between devices: none -> 70.9 us  [body(): lax.psum_scatter(natural_grads, 'dp', scatter_dimension=0, tiled=True)]
    unnamed x0 -> x1, blocking collectives: none -> 18.3 us
    all_gather x1, waiting for transfers between devices: 19.9 us -> 3.77 us  [body(): lax.all_gather(query_share, 'segment', axis=0, tiled=True)]
    reshape x4 -> x0, local copies, waits for them, and re-layouts: 8.91 us -> none  [the longest x1 2.78 us: body(): mixed_grads = jnp.transpose(natural_grads.reshape(groups, segments, passa...]
    all_gather x1 -> x2, blocking collectives: 36.7 us -> 39.3 us  [the longest x1 27.3 us: body(): passage_all = lax.all_gather(passage_group, 'dp', axis=0, tiled=True)]
    unnamed x69 -> x73, local copies, waits for them, and re-layouts: 10.2 us -> 9.75 us
  transfers between devices with their start and end apart: 6 -> 6, of which waited for: 6 -> 6; matrix products, arithmetic and copies ran while one was open for 7% -> 8% of each run, Pallas kernels for 0% -> 0%
where the time goes in v1:
time: 401 us; the launch traced here: 400 us
  waiting for transfers between devices  252 us (63%)
  blocking collectives  57.6 us (14%)
  matrix products  39.2 us (10%)
  other arithmetic  20.9 us (5%)
  between operations  15.2 us (4%)
  local copies, waits for them, and re-layouts  15.1 us (4%)
    reduce_scatter x1, waiting for transfers between devices, body(): lax.psum_scatter(weight_terms(), 'dp', scatter_dimension=0, tiled=True)  95.9 us
    reduce_scatter x1, waiting for transfers between devices, body(): lax.psum_scatter(natural_grads, 'dp', scatter_dimension=0, tiled=True)  70.9 us
    reduce_scatter x1, waiting for transfers between devices, body(): lax.psum_scatter(passage_parts[5], 'segment', scatter_dimension=0, tiled=...  36.7 us
    all_gather x1, blocking collectives, body(): passage_all = lax.all_gather(passage_group, 'dp', axis=0, tiled=True)  27.3 us
    reduce_scatter x1, waiting for transfers between devices, body(): lax.psum_scatter(query_parts[5], 'segment', scatter_dimension=0, tiled=True)  26.8 us
    unnamed x1, blocking collectives  18.3 us
    all_gather x1, waiting for transfers between devices, body(): lax.all_gather(passage_share, 'segment', axis=0, tiled=True)  17.5 us
    dot_general x6, matrix products, contract(): lax.dot_general(left, right, (((0,), (0,)), ((), ())), preferred_element_...  14.2 us
  transfers between devices with their start and end apart: 6, of which 6 were waited for; matrix products, arithmetic and copies ran while one was open for 8% of the time, Pallas kernels for 0%

profile of v1, /device:TPU:0, one launch (start us, length us, event | category | flops | bytes accessed | tf_op | source)
XLA Modules:
  0.0 400.1 jit_solution(18051587221549310980)
XLA Ops:
  7.2 0.8 slice_reduce_fusion.3
  8.1 1.9 fusion
  10.5 1.0 fusion.56
  11.6 0.8 copy-done.23
  12.5 2.6 multiply_convert_fusion.3
  15.0 1.0 copy-done.15
  16.0 2.6 fusion.50
  18.7 1.3 copy-done.3
  21.5 1.0 fusion.48
  22.9 3.0 multiply_convert_fusion.2
  25.9 3.9 fusion.42
  31.1 0.8 fusion.126
  31.9 0.8 fusion.124
  32.8 26.8 %reduce-scatter.5.cloned.1.call-done = f32[8,32,768]{2,1,0:T(8,128)} async-done(((f32[32,32,768]{2,1,0:T(8,128)}), f32[8,32,768]{2,1,0:T(8,128)}) %reduce-scatter.5.cloned.1.call-update) | async-done | bytes 786448 | tf_op jit(solution)/shard_map/reduce_scatter | solution.py:100
  59.6 1.5 multiply_reduce_fusion.5
  61.1 1.4 multiply_reduce_fusion.4
  62.5 0.7 multiply_reduce_fusion.6
  63.3 36.7 %reduce-scatter.7.cloned.1.call-done = f32[4,64,768]{2,1,0:T(8,128)} async-done(((f32[16,64,768]{2,1,0:T(8,128)}), f32[4,64,768]{2,1,0:T(8,128)}) %reduce-scatter.7.cloned.1.call-update) | async-done | bytes 786448 | tf_op jit(solution)/shard_map/reduce_scatter | solution.py:101
  100.0 1.5 multiply_reduce_fusion.3
  101.5 1.4 multiply_reduce_fusion.2
  102.9 0.7 multiply_reduce_fusion.8
  103.7 12.0 %all-gather = bf16[4,4,768]{2,1,0:T(4,128)(2,1)S(1)} all-gather(bf16[1,4,768]{2,1,0:T(4,128)(2,1)S(1)} %fusion.91), channel_id=1, replica_groups=mesh['segment'=4,'dp'=32] {'segment'}, dimensions={0}, use_global_device_ids=true | all-gather | bytes 30720 | tf_op jit(solution)/shard_map/all_gather | solution.py:113
  115.7 27.3 %all_gather.13 = bf16[512,768]{1,0:T(8,128)(2,1)} all-gather(bf16[16,768]{1,0:T(8,128)(2,1)S(1)} %reshape.215), channel_id=1, replica_groups=mesh['segment'=4,'dp'=32] {'dp'}, dimensions={0}, use_global_device_ids=true | all-gather | bytes 811008 | tf_op jit(solution)/shard_map/all_gather | solution.py:114
  143.1 2.2 gather_fusion
  146.0 2.0 fusion.74
  148.7 2.3 fusion.28
  151.4 1.0 fusion.40
  153.7 70.9 %reduce-scatter.9.cloned.1.call-done = f32[16,768]{1,0:T(8,128)} async-done(((f32[512,768]{1,0:T(8,128)}), f32[16,768]{1,0:T(8,128)}) %reduce-scatter.9.cloned.1.call-update) | async-done | bytes 49168 | tf_op jit(solution)/shard_map/reduce_scatter | solution.py:131
  224.7 18.3 %all-reduce.2 = f32[16,768]{1,0:T(8,128)S(1)} all-reduce(f32[16,768]{1,0:T(8,128)} %reduce-scatter.9.cloned.1.call-done), channel_id=5, replica_groups=mesh['segment'=4,'dp'=32] {'segment'}, use_global_device_ids=true, to_apply=%region_17.0.clone | all-reduce | flops 12288 | bytes 98304
  243.1 2.4 fusion.31
  245.5 1.5 multiply_reduce_fusion
  247.0 1.1 fusion.41
  248.2 3.8 all-gather.4.cloned.1.call-done
  251.9 3.7 convolution_bitcast_fusion.1
  255.7 1.0 fusion.52
  257.7 1.1 convolution_bitcast_fusion.3
  259.3 3.1 convolution_bitcast_fusion.5
  262.4 17.5 %all-gather.6.cloned.1.call-done = bf16[16,64,768]{2,1,0:T(8,128)(2,1)} async-done(((bf16[4,64,768]{2,1,0:T(8,128)(2,1)}), bf16[16,64,768]{2,1,0:T(8,128)(2,1)}) %all-gather.6.cloned.1.call-update) | async-done | bytes 1572880 | tf_op jit(solution)/shard_map/all_gather | solution.py:137
  279.9 2.8 convolution_bitcast_fusion
  282.7 1.0 fusion.44
  284.1 0.7 copy-done.32
  284.8 1.1 convolution_bitcast_fusion.2
  286.4 2.4 convolution_bitcast_fusion.4
  289.1 1.1 copy-done.9
  290.2 0.7 maximum_bitcast_fusion
  290.9 4.7 %pad_maximum_fusion = f32[768,3,2,512]{3,0,2,1:T(8,128)} fusion(f32[768,1,2,512]{3,0,2,1:T(8,128)S(1)} %maximum_bitcast_fusion.2, f32[768,1,2,512]{3,0,2,1:T(8,128)S(1)} %get-tuple-element.27, f32[768,1,2,512]{3,0,2,1:T(8,128)S(1)} %get-tuple-element.26), kind=kLoop, calls=%fused_computation.1 | loop fusion | flops 4718592 | bytes 18874368 | tf_op jit(solution)/shard_map/stack | solution.py:164
  295.7 95.9 %reduce-scatter.11.cloned.1.call-done = f32[24,3,2,512]{3,0,2,1:T(8,128)} async-done(((f32[768,3,2,512]{3,0,2,1:T(8,128)}), f32[24,3,2,512]{3,0,2,1:T(8,128)}) %reduce-scatter.11.cloned.1.call-update) | async-done | bytes 294928 | tf_op jit(solution)/shard_map/reduce_scatter | solution.py:166
  391.5 1.7 slice_bitcast_fusion
  (120 shorter events, 9.3 us)
Async XLA Ops:
  7.2 23.6 %copy-start = (s32[32,15]{0,1:T(8,128)S(1)}, s32[32,15]{0,1:T(8,128)}, u32[]{:S(2)}) copy-start(s32[32,15]{0,1:T(8,128)} %param.24) | copy-start | bytes 5764
  7.2 2.8 copy-start.2
  7.2 52.4 %reduce-scatter.5.cloned.1.call-start = ((), (), s32[]{:S(2)}) async-start(), calls=%async_computation.4 | async-start | bytes 3932160 | tf_op jit(solution)/shard_map/reduce_scatter | solution.py:100
  8.1 2.4 copy-start.21
  10.5 1.2 copy-start.10
  10.5 2.0 copy-start.23
  12.5 2.6 copy-start.29
  12.5 3.6 copy-start.6
  15.0 1.0 copy-start.15
  18.7 1.4 copy-start.3
  18.7 81.3 %reduce-scatter.7.cloned.1.call-start = ((), (), s32[]{:S(2)}) async-start(), calls=%async_computation.5 | async-start | bytes 3932160 | tf_op jit(solution)/shard_map/reduce_scatter | solution.py:101
  20.1 1.4 copy-start.22
  20.9 1.6 copy-start.12
  21.5 1.4 copy-start.24
  22.9 3.0 copy-start.31
  22.9 3.0 copy-start.7
  29.8 0.7 copy-start.27
  29.8 0.7 copy-start.18
  29.8 3.0 copy-start.17
  29.8 194.8 %reduce-scatter.9.cloned.1.call-start = ((), (), s32[]{:S(2)}) async-start(), calls=%async_computation.7 | async-start | bytes 1622016 | tf_op jit(solution)/shard_map/reduce_scatter | solution.py:131
  59.6 2.9 copy-start.19
  100.0 2.9 copy-start.20
  148.1 103.8 %all-gather.4.cloned.1.call-start = ((), (), s32[]{:S(2)}) async-start(), calls=%async_computation.6 | async-start | bytes 1966080 | tf_op jit(solution)/shard_map/all_gather | solution.py:136
  148.3 2.7 copy-start.4
  148.7 3.8 copy-start.28
  152.4 94.6 %copy-start.5 = (f32[4,64,768]{2,1,0:T(8,128)S(1)}, f32[4,64,768]{2,1,0:T(8,128)}, u32[]{:S(2)}) copy-start(f32[4,64,768]{2,1,0:T(8,128)} %reduce-scatter.7.cloned.1.call-done) | copy-start | bytes 2359300
  152.4 127.5 %all-gather.6.cloned.1.call-start = ((), (), s32[]{:S(2)}) async-start(), calls=%async_computation.8 | async-start | bytes 1966080 | tf_op jit(solution)/shard_map/all_gather | solution.py:137
  243.1 8.8 %copy-start.16 = (bf16[1024,512]{1,0:T(8,128)(2,1)S(1)}, bf16[1024,512]{1,0:T(8,128)(2,1)}, u32[]{:S(2)}) copy-start(bf16[1024,512]{1,0:T(8,128)(2,1)} %copy-done.15) | copy-start | bytes 3145732
  248.1 143.4 %reduce-scatter.11.cloned.1.call-start = ((), (), s32[]{:S(2)}) async-start(), calls=%async_computation.9 | async-start | bytes 9732096 | tf_op jit(solution)/shard_map/reduce_scatter | solution.py:166
  251.9 3.7 copy-start.8
  251.9 3.7 copy-start.25
  255.7 1.4 copy-start.11
  255.7 2.1 copy-start.30
  257.7 1.6 copy-start.33
  279.9 2.8 copy-start.26
  282.7 1.4 copy-start.13
  282.7 2.1 copy-start.32
  284.8 1.6 copy-start.34
  286.4 2.4 copy-start.14
  288.8 1.4 copy-start.9
  295.7 97.6 %copy-start.1 = (s32[32,15]{0,1:T(8,128)S(1)}, s32[32,15]{0,1:T(8,128)}, u32[]{:S(2)}) copy-start(s32[32,15]{0,1:T(8,128)} %param.24) | copy-start | bytes 5764
Sparse Core Ops, SparseCore 0:
  18.8 40.7 reduce-scatter.4
  62.0 37.9 reduce-scatter.6
  148.2 76.4 reduce-scatter.8
  226.2 25.7 all-gather.3
  253.4 26.4 all-gather.5
  295.8 95.7 reduce-scatter.10

commit v2 on v1

--- a/solution.py
+++ b/solution.py
@@ -110,26 +110,57 @@
     )
     query_round = query_embed.astype(jnp.bfloat16)
     passage_round = passage_embed.astype(jnp.bfloat16)
-    passage_group = lax.all_gather(passage_round, "segment", axis=0, tiled=True)
-    passage_all = lax.all_gather(passage_group, "dp", axis=0, tiled=True)
-    cand_ids = jnp.concatenate(
+    id_radix = 256
+    own_ids = jnp.concatenate(
         [own_rows(positive_ids, query_dev)[:, None], own_rows(negative_ids, query_dev)], axis=1
     )
-    cand_rows = passage_all[cand_ids]
-    scores = jnp.einsum("qd,qcd->qc", query_round, cand_rows, preferred_element_type=jnp.float32)
-    score_grads = score_grads_of(scores, own_rows(negative_counts, query_dev))
-    query_grad = jnp.einsum(
-        "qc,qcd->qd", score_grads, cand_rows.astype(jnp.float32), precision=lax.Precision.HIGHEST
-    )
+    slots = own_ids.shape[1]
+    own_meta = jnp.concatenate(
+        [own_ids // id_radix, own_ids % id_radix, own_rows(negative_counts, query_dev)[:, None]],
+        axis=1,
+    ).astype(jnp.bfloat16)
+    meta_width = own_meta.shape[1]
+    meta_rows = -(-query_dev * meta_width // model_width)
+    meta_flat = jnp.pad(
+        own_meta.reshape(-1), (0, meta_rows * model_width - query_dev * meta_width)
+    ).reshape(meta_rows, model_width)
+    packed = jnp.concatenate([query_round, passage_round, meta_flat], axis=0)
+    gathered = lax.all_gather(packed, ("dp", "segment"), axis=0, tiled=False)
+    gathered = gathered.reshape(groups, segments, -1, model_width)
+    query_all = gathered[:, :, :query_dev].reshape(-1, model_width)
+    passage_all = gathered[:, :, query_dev : query_dev + passage_dev].reshape(-1, model_width)
+    meta_all = (
+        gathered[:, :, query_dev + passage_dev :]
+        .reshape(groups, segments, -1)[:, :, : query_dev * meta_width]
+        .reshape(-1, meta_width)
+        .astype(jnp.int32)
+    )
+    cand_all = meta_all[:, :slots] * id_radix + meta_all[:, slots : 2 * slots]
+    counts_all = meta_all[:, 2 * slots]
     passage_total = passage_all.shape[0]
+    all_scores = lax.dot_general(
+        query_all, passage_all, (((1,), (1,)), ((), ())), preferred_element_type=jnp.float32
+    )
     every_id = lax.broadcasted_iota(jnp.int32, (1, 1, passage_total), 2)
-    matches = (cand_ids[:, :, None] == every_id).astype(jnp.float32)
-    coefficient = jnp.einsum("qcp,qc->pq", matches, score_grads, precision=lax.Precision.HIGHEST)
-    natural_grads = jnp.dot(
-        coefficient, query_round.astype(jnp.float32), precision=lax.Precision.HIGHEST
-    )
-    group_grads = lax.psum_scatter(natural_grads, "dp", scatter_dimension=0, tiled=True)
-    passage_grad = lax.psum_scatter(group_grads, "segment", scatter_dimension=0, tiled=True)
+    matches = cand_all[:, :, None] == every_id
+    scores = jnp.sum(jnp.where(matches, all_scores[:, None, :], 0.0), axis=2)
+    score_grads = score_grads_of(scores, counts_all)
+    coefficient = jnp.sum(jnp.where(matches, score_grads[:, :, None], 0.0), axis=1)
+    dp_index = lax.axis_index("dp")
+    query_start = (dp_index * segments + segment_index) * query_dev
+    passage_start = (dp_index * segments + segment_index) * passage_dev
+    query_coef = lax.dynamic_slice_in_dim(coefficient, query_start, query_dev, 0)
+    passage_coef = lax.dynamic_slice_in_dim(coefficient, passage_start, passage_dev, 1)
+    query_grad = jnp.dot(
+        query_coef, passage_all.astype(jnp.float32), precision=lax.Precision.HIGHEST
+    )
+    passage_grad = lax.dot_general(
+        passage_coef,
+        query_all.astype(jnp.float32),
+        (((0,), (0,)), ((), ())),
+        precision=lax.Precision.HIGHEST,
+        preferred_element_type=jnp.float32,
+    )
     query_share = query_back(query_grad)[0].astype(jnp.bfloat16)
     passage_share = passage_back(passage_grad)[0].astype(jnp.bfloat16)
     query_rows, passage_rows = (

time: 401 us -> 386 us (0.963)
  blocking collectives: 57.6 us -> 0 us
  other arithmetic: 20.9 us -> 42.3 us
  waiting for transfers between devices: 252 us -> 264 us
  local copies, waits for them, and re-layouts: 15.1 us -> 22.8 us
    reduce_scatter x1 -> x0, waiting for transfers between devices: 70.9 us -> none  [body(): lax.psum_scatter(natural_grads, 'dp', scatter_dimension=0, tiled=True)]
    all_gather x0 -> x1, waiting for transfers between devices: none -> 65.5 us  [body(): gathered = lax.all_gather(packed, ('dp', 'segment'), axis=0, tiled=False)]
    all_gather x2 -> x0, blocking collectives: 39.3 us -> none  [the longest x1 27.3 us: body(): passage_all = lax.all_gather(passage_group, 'dp', axis=0, tiled=True)]
    unnamed x1 -> x0, blocking collectives: 18.3 us -> none
    reduce_sum x2, other arithmetic: 0.25 us -> 16.4 us  [the longest x1 9.56 us: body(): jnp.sum(jnp.where(matches, score_grads[:, :, None], 0.0), axis=1)]
    all_gather x1, waiting for transfers between devices: 3.77 us -> 17.1 us  [body(): lax.all_gather(query_share, 'segment', axis=0, tiled=True)]
    slice x0 -> x6, local copies, waits for them, and re-layouts: none -> 7.43 us  [the longest x1 2.5 us: body(): gathered[:, :, query_dev:query_dev + passage_dev].reshape(-1, model_width)]
    all_gather x1, waiting for transfers between devices: 17.5 us -> 21.6 us  [body(): lax.all_gather(passage_share, 'segment', axis=0, tiled=True)]
  transfers between devices with their start and end apart: 6 -> 6, of which waited for: 6 -> 6; matrix products, arithmetic and copies ran while one was open for 8% -> 7% of each run, Pallas kernels for 0% -> 0%
where the time goes in v2:
time: 386 us; the launch traced here: 385 us
  waiting for transfers between devices  264 us (68%)
  other arithmetic  42.3 us (11%)
  matrix products  40.3 us (10%)
  local copies, waits for them, and re-layouts  22.8 us (6%)
  between operations  14.6 us (4%)
    reduce_scatter x1, waiting for transfers between devices, body(): lax.psum_scatter(weight_terms(), 'dp', scatter_dimension=0, tiled=True)  95.9 us
    all_gather x1, waiting for transfers between devices, body(): gathered = lax.all_gather(packed, ('dp', 'segment'), axis=0, tiled=False)  65.5 us
    reduce_scatter x1, waiting for transfers between devices, body(): lax.psum_scatter(passage_parts[5], 'segment', scatter_dimension=0, tiled=...  36.7 us
    reduce_scatter x1, waiting for transfers between devices, body(): lax.psum_scatter(query_parts[5], 'segment', scatter_dimension=0, tiled=True)  27.4 us
    all_gather x1, waiting for transfers between devices, body(): lax.all_gather(passage_share, 'segment', axis=0, tiled=True)  21.6 us
    all_gather x1, waiting for transfers between devices, body(): lax.all_gather(query_share, 'segment', axis=0, tiled=True)  17.1 us
    dot_general x6, matrix products, contract(): lax.dot_general(left, right, (((0,), (0,)), ((), ())), preferred_element_...  13.6 us
    reduce_sum x1, other arithmetic, body(): jnp.sum(jnp.where(matches, score_grads[:, :, None], 0.0), axis=1)  9.56 us
  transfers between devices with their start and end apart: 6, of which 6 were waited for; matrix products, arithmetic and copies ran while one was open for 7% of the time, Pallas kernels for 0%

profile of v2, /device:TPU:0, one launch (start us, length us, event | category | flops | bytes accessed | tf_op | source)
XLA Modules:
  0.0 385.0 jit_solution(17463517384495858346)
XLA Ops:
  8.1 1.9 fusion
  10.5 1.0 fusion.56
  12.5 2.6 multiply_convert_fusion.3
  15.1 1.0 copy-done.18
  16.1 2.6 fusion.50
  18.8 1.3 copy-done.3
  21.5 1.0 fusion.48
  23.0 2.6 multiply_convert_fusion.2
  25.5 1.0 copy-done.19
  26.5 2.7 fusion.42
  32.2 27.4 %reduce-scatter.4.cloned.1.call-done = f32[8,32,768]{2,1,0:T(8,128)} async-done(((f32[32,32,768]{2,1,0:T(8,128)}), f32[8,32,768]{2,1,0:T(8,128)}) %reduce-scatter.4.cloned.1.call-update) | async-done | bytes 786448 | tf_op jit(solution)/shard_map/reduce_scatter | solution.py:100
  59.6 1.5 multiply_reduce_fusion.5
  61.1 1.4 multiply_reduce_fusion.4
  63.3 36.7 %reduce-scatter.6.cloned.1.call-done = f32[4,64,768]{2,1,0:T(8,128)} async-done(((f32[16,64,768]{2,1,0:T(8,128)}), f32[4,64,768]{2,1,0:T(8,128)}) %reduce-scatter.6.cloned.1.call-update) | async-done | bytes 786448 | tf_op jit(solution)/shard_map/reduce_scatter | solution.py:101
  100.1 1.5 multiply_reduce_fusion.3
  101.5 1.4 multiply_reduce_fusion.2
  104.7 65.5 %all-gather.10.cloned.1.call-done = bf16[128,13,768]{2,1,0:T(8,128)(2,1)} async-done(((bf16[1,13,768]{2,1,0:T(8,128)(2,1)}), bf16[128,13,768]{2,1,0:T(8,128)(2,1)}) %all-gather.10.cloned.1.call-update) | async-done | bytes 2555920 | tf_op jit(solution)/shard_map/all_gather | solution.py:128
  170.3 1.8 slice.98
  172.3 1.0 reshape.148
  173.4 1.6 slice_reduce_fusion.1
  174.9 2.2 slice_add_fusion
  177.1 2.5 slice.104
  179.6 1.3 slice.103
  180.9 2.2 reshape.145
  183.2 2.7 fusion.126
  185.8 6.8 %select_reduce_fusion.1 = f32[1024,16]{1,0:T(8,128)S(1)} fusion(f32[1024,512]{1,0:T(8,128)S(1)} %fusion.126, s32[1024,16]{1,0:T(8,128)S(1)} %copy-done.6), kind=kLoop, calls=%fused_computation.1 | loop fusion | flops 25149440 | bytes 2228224 | tf_op jit(solution)/shard_map/reduce_sum | solution.py:146
  193.5 1.6 fusion.120
  195.1 1.0 copy.42
  196.2 1.5 pad_add_fusion
  197.7 9.6 %select_reduce_fusion = f32[1024,512]{1,0:T(8,128)S(1)} fusion(f32[1024,16]{1,0:T(8,128)S(1)} %pad_add_fusion, s32[1024,16]{1,0:T(8,128)} %slice_add_fusion), kind=kLoop, calls=%fused_computation | loop fusion | flops 24641536 | bytes 2228224 | tf_op jit(solution)/shard_map/reduce_sum | solution.py:148
  207.8 1.0 fusion.28
  209.2 1.1 fusion.40
  210.3 2.8 multiply_reduce_fusion.8
  213.2 2.3 fusion.31
  215.8 1.1 fusion.41
  217.2 17.1 %all-gather.6.cloned.1.call-done = bf16[32,32,768]{2,1,0:T(8,128)(2,1)} async-done(((bf16[8,32,768]{2,1,0:T(8,128)(2,1)}), bf16[32,32,768]{2,1,0:T(8,128)(2,1)}) %all-gather.6.cloned.1.call-update) | async-done | bytes 1572880 | tf_op jit(solution)/shard_map/all_gather | solution.py:167
  234.3 4.0 %convolution_bitcast_fusion.1 = f32[768,1,512]{2,0,1:T(8,128)} fusion(bf16[1024,768]{1,0:T(8,128)(2,1)} %bitcast.131, bf16[1024,512]{1,0:T(8,128)(2,1)} %copy-done.18), kind=kOutput, calls=%fused_computation.42 | convolution fusion | flops 805306368 | bytes 4194304 | tf_op jit(solution)/shard_map/dot_general | solution.py:37
  238.3 2.4 fusion.52
  240.6 21.6 %all-gather.8.cloned.1.call-done = bf16[16,64,768]{2,1,0:T(8,128)(2,1)} async-done(((bf16[4,64,768]{2,1,0:T(8,128)(2,1)}), bf16[16,64,768]{2,1,0:T(8,128)(2,1)}) %all-gather.8.cloned.1.call-update) | async-done | bytes 1572880 | tf_op jit(solution)/shard_map/all_gather | solution.py:168
  262.3 2.6 convolution_bitcast_fusion
  264.9 1.0 fusion.44
  266.9 1.1 convolution_bitcast_fusion.3
  268.5 2.4 convolution_bitcast_fusion.5
  270.9 1.1 convolution_bitcast_fusion.2
  272.5 2.4 convolution_bitcast_fusion.4
  275.8 4.7 %pad_maximum_fusion = f32[768,3,2,512]{3,0,2,1:T(8,128)} fusion(f32[768,1,2,512]{3,0,2,1:T(8,128)S(1)} %maximum_bitcast_fusion.2, f32[768,1,2,512]{3,0,2,1:T(8,128)S(1)} %maximum_bitcast_fusion.1, f32[768,1,2,512]{3,0,2,1:T(8,128)S(1)} %maximum_bitcast_fusion), kind=kLoop, calls=%fused_computation.3 | loop fusion | flops 4718592 | bytes 18874368 | tf_op jit(solution)/shard_map/stack | solution.py:195
  280.6 95.9 %reduce-scatter.8.cloned.1.call-done = f32[24,3,2,512]{3,0,2,1:T(8,128)} async-done(((f32[768,3,2,512]{3,0,2,1:T(8,128)}), f32[24,3,2,512]{3,0,2,1:T(8,128)}) %reduce-scatter.8.cloned.1.call-update) | async-done | bytes 294928 | tf_op jit(solution)/shard_map/reduce_scatter | solution.py:197
  376.5 1.7 slice_bitcast_fusion
  (134 shorter events, 15.3 us)
Async XLA Ops:
  7.2 23.0 %copy-start = (s32[32,15]{0,1:T(8,128)S(1)}, s32[32,15]{0,1:T(8,128)}, u32[]{:S(2)}) copy-start(s32[32,15]{0,1:T(8,128)} %param.24) | copy-start | bytes 5764
  7.2 2.8 copy-start.2
  7.2 52.5 %reduce-scatter.4.cloned.1.call-start = ((), (), s32[]{:S(2)}) async-start(), calls=%async_computation.3 | async-start | bytes 3932160 | tf_op jit(solution)/shard_map/reduce_scatter | solution.py:100
  8.1 2.4 copy-start.27
  10.5 1.2 copy-start.13
  10.5 2.0 copy-start.29
  12.5 2.6 copy-start.34
  12.5 3.6 copy-start.10
  15.1 1.0 copy-start.18
  18.7 1.4 copy-start.3
  18.7 81.3 %reduce-scatter.6.cloned.1.call-start = ((), (), s32[]{:S(2)}) async-start(), calls=%async_computation.4 | async-start | bytes 3932160 | tf_op jit(solution)/shard_map/reduce_scatter | solution.py:101
  20.1 1.4 copy-start.28
  21.0 1.6 copy-start.15
  21.5 1.4 copy-start.30
  22.9 2.6 copy-start.36
  22.9 3.6 copy-start.11
  25.5 1.0 copy-start.19
  29.2 0.7 copy-start.22
  29.2 0.7 copy-start.23
  29.2 3.0 copy-start.21
  29.2 141.0 %all-gather.10.cloned.1.call-start = ((), (), s32[]{:S(2)}) async-start(), calls=%async_computation.8 | async-start | bytes 3170304 | tf_op jit(solution)/shard_map/all_gather | solution.py:128
  59.6 2.9 copy-start.24
  100.1 2.9 copy-start.25
  104.5 129.8 %all-gather.6.cloned.1.call-start = ((), (), s32[]{:S(2)}) async-start(), calls=%async_computation.5 | async-start | bytes 1966080 | tf_op jit(solution)/shard_map/all_gather | solution.py:167
  173.3 6.3 %copy-start.9 = (bf16[128,13,768]{2,1,0:T(8,128)(2,1)S(1)}, bf16[128,13,768]{2,1,0:T(8,128)(2,1)}, u32[]{:S(2)}) copy-start(bf16[128,13,768]{2,1,0:T(8,128)(2,1)} %all-gather.10.cloned.1.call-done) | copy-start | bytes 7667716
  183.2 2.7 copy-start.6
  196.2 11.1 %copy-start.8 = (bf16[512,768]{1,0:T(8,128)(2,1)S(1)}, bf16[512,768]{1,0:T(8,128)(2,1)}, u32[]{:S(2)}) copy-start(bf16[512,768]{1,0:T(8,128)(2,1)} %reshape.145) | copy-start | bytes 2359300
  197.6 10.2 %copy-start.26 = (bf16[2,768,768]{2,1,0:T(8,128)(2,1)S(1)}, bf16[2,768,768]{2,1,0:T(8,128)(2,1)}, u32[]{:S(2)}) copy-start(bf16[2,768,768]{2,1,0:T(8,128)(2,1)} %param.22) | copy-start | bytes 7077892
  197.6 11.2 %copy-start.4 = (f32[8,32,768]{2,1,0:T(8,128)S(1)}, f32[8,32,768]{2,1,0:T(8,128)}, u32[]{:S(2)}) copy-start(f32[8,32,768]{2,1,0:T(8,128)} %reduce-scatter.4.cloned.1.call-done) | copy-start | bytes 2359300
  207.2 2.0 copy-start.7
  210.3 5.2 %copy-start.5 = (f32[4,64,768]{2,1,0:T(8,128)S(1)}, f32[4,64,768]{2,1,0:T(8,128)}, u32[]{:S(2)}) copy-start(f32[4,64,768]{2,1,0:T(8,128)} %reduce-scatter.6.cloned.1.call-done) | copy-start | bytes 2359300
  210.3 52.0 %all-gather.8.cloned.1.call-start = ((), (), s32[]{:S(2)}) async-start(), calls=%async_computation.6 | async-start | bytes 1966080 | tf_op jit(solution)/shard_map/all_gather | solution.py:168
  216.9 159.6 %reduce-scatter.8.cloned.1.call-start = ((), (), s32[]{:S(2)}) async-start(), calls=%async_computation.7 | async-start | bytes 9732096 | tf_op jit(solution)/shard_map/reduce_scatter | solution.py:197
  234.3 4.0 %copy-start.12 = (bf16[2,512,768]{2,1,0:T(8,128)(2,1)S(1)}, bf16[2,512,768]{2,1,0:T(8,128)(2,1)}, u32[]{:S(2)}) copy-start(bf16[2,512,768]{2,1,0:T(8,128)(2,1)} %param.21) | copy-start | bytes 4718596
  234.3 4.0 %copy-start.31 = (bf16[32,32,768]{2,1,0:T(8,128)(2,1)S(1)}, bf16[32,32,768]{2,1,0:T(8,128)(2,1)}, u32[]{:S(2)}) copy-start(bf16[32,32,768]{2,1,0:T(8,128)(2,1)} %all-gather.6.cloned.1.call-done) | copy-start | bytes 4718596
  238.3 24.0 %copy-start.20 = (bf16[1024,512]{1,0:T(8,128)(2,1)S(1)}, bf16[1024,512]{1,0:T(8,128)(2,1)}, u32[]{:S(2)}) copy-start(bf16[1024,512]{1,0:T(8,128)(2,1)} %copy-done.19) | copy-start | bytes 3145732
  262.3 2.6 copy-start.32
  262.3 3.6 copy-start.35
  264.8 1.4 copy-start.14
  264.8 2.1 copy-start.33
  266.9 1.6 copy-start.38
  268.5 2.4 copy-start.16
  268.5 2.4 copy-start.37
  270.9 1.6 copy-start.39
  272.5 2.4 copy-start.17
  280.6 97.6 %copy-start.1 = (s32[32,15]{0,1:T(8,128)S(1)}, s32[32,15]{0,1:T(8,128)}, u32[]{:S(2)}) copy-start(s32[32,15]{0,1:T(8,128)} %param.24) | copy-start | bytes 5764
Sparse Core Ops, SparseCore 0:
  18.9 40.7 reduce-scatter.3
  62.1 37.9 reduce-scatter.5
  104.6 65.5 all-gather.9
  210.4 23.8 all-gather.5
  235.8 26.4 all-gather.7
  280.7 95.7 reduce-scatter.7

commit v3 on v2

--- a/solution.py
+++ b/solution.py
@@ -141,16 +141,21 @@
     all_scores = lax.dot_general(
         query_all, passage_all, (((1,), (1,)), ((), ())), preferred_element_type=jnp.float32
     )
-    every_id = lax.broadcasted_iota(jnp.int32, (1, 1, passage_total), 2)
-    matches = cand_all[:, :, None] == every_id
-    scores = jnp.sum(jnp.where(matches, all_scores[:, None, :], 0.0), axis=2)
+    scores = jnp.take_along_axis(all_scores, cand_all, axis=1)
     score_grads = score_grads_of(scores, counts_all)
-    coefficient = jnp.sum(jnp.where(matches, score_grads[:, :, None], 0.0), axis=1)
     dp_index = lax.axis_index("dp")
     query_start = (dp_index * segments + segment_index) * query_dev
     passage_start = (dp_index * segments + segment_index) * passage_dev
-    query_coef = lax.dynamic_slice_in_dim(coefficient, query_start, query_dev, 0)
-    passage_coef = lax.dynamic_slice_in_dim(coefficient, passage_start, passage_dev, 1)
+    own_cand = lax.dynamic_slice_in_dim(cand_all, query_start, query_dev, 0)
+    own_grads = lax.dynamic_slice_in_dim(score_grads, query_start, query_dev, 0)
+    every_id = lax.broadcasted_iota(jnp.int32, (1, 1, passage_total), 2)
+    query_coef = jnp.sum(
+        jnp.where(own_cand[:, :, None] == every_id, own_grads[:, :, None], 0.0), axis=1
+    )
+    own_passages = passage_start + lax.broadcasted_iota(jnp.int32, (1, 1, passage_dev), 2)
+    passage_coef = jnp.sum(
+        jnp.where(cand_all[:, :, None] == own_passages, score_grads[:, :, None], 0.0), axis=1
+    )
     query_grad = jnp.dot(
         query_coef, passage_all.astype(jnp.float32), precision=lax.Precision.HIGHEST
     )

time: 386 us -> 497 us (1.29)
  local copies, waits for them, and re-layouts: 22.8 us -> 150 us
  other arithmetic: 42.3 us -> 25.1 us
    gather x0 -> x3, local copies, waits for them, and re-layouts: none -> 130 us  [body(): scores = jnp.take_along_axis(all_scores, cand_all, axis=1)]
    reduce_sum x2, other arithmetic: 16.4 us -> 0.27 us  [the longest x1 0.14 us: body(): jnp.sum(jnp.where(own_cand[:, :, None] == every_id, own_grads[:, :, None]...]
  transfers between devices with their start and end apart: 6 -> 6, of which waited for: 6 -> 6; matrix products, arithmetic and copies ran while one was open for 7% -> 5% of each run, Pallas kernels for 0% -> 0%
where the time goes in v3:
time: 497 us; the launch traced here: 496 us
  waiting for transfers between devices  264 us (53%)
  local copies, waits for them, and re-layouts  150 us (30%)
  matrix products  41.1 us (8%)
  other arithmetic  25.1 us (5%)
  between operations  15.2 us (3%)
    gather x3, local copies, waits for them, and re-layouts, body(): scores = jnp.take_along_axis(all_scores, cand_all, axis=1)  130 us
    reduce_scatter x1, waiting for transfers between devices, body(): lax.psum_scatter(weight_terms(), 'dp', scatter_dimension=0, tiled=True)  95.9 us
    all_gather x1, waiting for transfers between devices, body(): gathered = lax.all_gather(packed, ('dp', 'segment'), axis=0, tiled=False)  65.5 us
    reduce_scatter x1, waiting for transfers between devices, body(): lax.psum_scatter(passage_parts[5], 'segment', scatter_dimension=0, tiled=...  36.7 us
    reduce_scatter x1, waiting for transfers between devices, body(): lax.psum_scatter(query_parts[5], 'segment', scatter_dimension=0, tiled=True)  27.3 us
    all_gather x1, waiting for transfers between devices, body(): lax.all_gather(passage_share, 'segment', axis=0, tiled=True)  22.7 us
    all_gather x1, waiting for transfers between devices, body(): lax.all_gather(query_share, 'segment', axis=0, tiled=True)  15.6 us
    dot_general x6, matrix products, contract(): lax.dot_general(left, right, (((0,), (0,)), ((), ())), preferred_element_...  12.7 us
  transfers between devices with their start and end apart: 6, of which 6 were waited for; matrix products, arithmetic and copies ran while one was open for 5% of the time, Pallas kernels for 0%

profile of v3, /device:TPU:0, one launch (start us, length us, event | category | flops | bytes accessed | tf_op | source)
XLA Modules:
  0.0 496.1 jit_solution(10540428919395859232)
XLA Ops:
  7.2 0.8 slice_reduce_fusion.5
  8.1 1.9 fusion
  10.5 1.0 fusion.56
  12.5 2.6 multiply_convert_fusion.3
  15.1 1.0 copy-done.18
  16.1 2.6 fusion.50
  18.8 1.3 copy-done.4
  21.5 1.0 fusion.48
  22.9 2.6 multiply_convert_fusion.2
  25.6 1.0 copy-done.19
  26.5 2.6 fusion.42
  32.3 27.3 %reduce-scatter.4.cloned.1.call-done = f32[8,32,768]{2,1,0:T(8,128)} async-done(((f32[32,32,768]{2,1,0:T(8,128)}), f32[8,32,768]{2,1,0:T(8,128)}) %reduce-scatter.4.cloned.1.call-update) | async-done | bytes 786448 | tf_op jit(solution)/shard_map/reduce_scatter | solution.py:100
  59.6 1.5 multiply_reduce_fusion.5
  61.1 1.4 multiply_reduce_fusion.4
  63.4 36.7 %reduce-scatter.6.cloned.1.call-done = f32[4,64,768]{2,1,0:T(8,128)} async-done(((f32[16,64,768]{2,1,0:T(8,128)}), f32[4,64,768]{2,1,0:T(8,128)}) %reduce-scatter.6.cloned.1.call-update) | async-done | bytes 786448 | tf_op jit(solution)/shard_map/reduce_scatter | solution.py:101
  100.0 1.5 multiply_reduce_fusion.3
  101.6 1.4 multiply_reduce_fusion.2
  105.3 65.5 %all-gather.10.cloned.1.call-done = bf16[128,13,768]{2,1,0:T(8,128)(2,1)} async-done(((bf16[1,13,768]{2,1,0:T(8,128)(2,1)}), bf16[128,13,768]{2,1,0:T(8,128)(2,1)}) %all-gather.10.cloned.1.call-update) | async-done | bytes 2555920 | tf_op jit(solution)/shard_map/all_gather | solution.py:128
  170.8 1.8 slice.100
  173.2 1.0 slice_reduce_fusion.1
  174.1 1.0 bitcast_or_fusion
  175.2 1.6 slice.106
  176.8 1.3 slice.105
  178.5 0.9 copy-done.9
  179.4 2.4 fusion.121
  181.8 129.5 %gather_fusion = f32[16384]{0:T(1024)S(1)} fusion(f32[1024,512]{1,0:T(8,128)S(1)} %fusion.121, s32[16384]{0:T(1024)S(1)} %reshape.165), kind=kCustom, calls=%fused_computation | custom fusion | bytes 262144 | tf_op jit(solution)/shard_map/jit(take_along_axis)/gather | solution.py:144
  312.6 1.0 fusion.115
  313.6 1.0 copy.42
  315.6 1.7 multiply_reduce_fusion.6
  317.3 2.3 fusion.28
  320.0 1.0 fusion.40
  321.3 1.3 pad_add_fusion
  322.9 2.4 multiply_reduce_fusion.8
  325.4 2.3 fusion.31
  328.1 1.1 fusion.41
  329.5 15.6 %all-gather.6.cloned.1.call-done = bf16[32,32,768]{2,1,0:T(8,128)(2,1)} async-done(((bf16[8,32,768]{2,1,0:T(8,128)(2,1)}), bf16[32,32,768]{2,1,0:T(8,128)(2,1)}) %all-gather.6.cloned.1.call-update) | async-done | bytes 1572880 | tf_op jit(solution)/shard_map/all_gather | solution.py:172
  345.0 2.9 convolution_bitcast_fusion.1
  347.9 2.3 fusion.52
  350.3 22.7 %all-gather.8.cloned.1.call-done = bf16[16,64,768]{2,1,0:T(8,128)(2,1)} async-done(((bf16[4,64,768]{2,1,0:T(8,128)(2,1)}), bf16[16,64,768]{2,1,0:T(8,128)(2,1)}) %all-gather.8.cloned.1.call-update) | async-done | bytes 1572880 | tf_op jit(solution)/shard_map/all_gather | solution.py:173
  373.0 2.8 convolution_bitcast_fusion
  375.9 1.0 fusion.44
  377.9 1.1 convolution_bitcast_fusion.3
  379.5 2.4 convolution_bitcast_fusion.5
  381.9 1.1 convolution_bitcast_fusion.2
  383.5 2.4 convolution_bitcast_fusion.4
  386.8 4.8 pad_maximum_fusion
  391.7 95.9 %reduce-scatter.8.cloned.1.call-done = f32[24,3,2,512]{3,0,2,1:T(8,128)} async-done(((f32[768,3,2,512]{3,0,2,1:T(8,128)}), f32[24,3,2,512]{3,0,2,1:T(8,128)}) %reduce-scatter.8.cloned.1.call-update) | async-done | bytes 294928 | tf_op jit(solution)/shard_map/reduce_scatter | solution.py:202
  487.5 1.7 slice_bitcast_fusion
  (205 shorter events, 16.8 us)
Async XLA Ops:
  7.2 23.0 %copy-start = (s32[32,15]{0,1:T(8,128)S(1)}, s32[32,15]{0,1:T(8,128)}, u32[]{:S(2)}) copy-start(s32[32,15]{0,1:T(8,128)} %param.24) | copy-start | bytes 5764
  7.2 52.4 %reduce-scatter.4.cloned.1.call-start = ((), (), s32[]{:S(2)}) async-start(), calls=%async_computation.3 | async-start | bytes 3932160 | tf_op jit(solution)/shard_map/reduce_scatter | solution.py:100
  12.5 3.6 copy-start.11
  18.7 81.3 %reduce-scatter.6.cloned.1.call-start = ((), (), s32[]{:S(2)}) async-start(), calls=%async_computation.4 | async-start | bytes 3932160 | tf_op jit(solution)/shard_map/reduce_scatter | solution.py:101
  22.9 3.6 copy-start.12
  29.2 3.0 copy-start.41
  29.2 141.6 %all-gather.10.cloned.1.call-start = ((), (), s32[]{:S(2)}) async-start(), calls=%async_computation.8 | async-start | bytes 3170304 | tf_op jit(solution)/shard_map/all_gather | solution.py:128
  31.4 70.2 %copy-start.35 = (f32[4,64]{1,0:T(4,128)}, f32[4,64]{1,0:T(4,128)S(1)}, u32[]{:S(2)}) copy-start(f32[4,64]{1,0:T(4,128)S(1)} %get-tuple-element.14) | copy-start | bytes 3076
  31.4 71.6 %copy-start.46 = (f32[4]{0:T(128)}, f32[4]{0:T(128)S(1)}, u32[]{:S(2)}) copy-start(f32[4]{0:T(128)S(1)} %get-tuple-element.13) | copy-start | bytes 52
  32.2 69.3 %copy-start.26 = (f32[8,32]{1,0:T(8,128)}, f32[8,32]{1,0:T(8,128)S(1)}, u32[]{:S(2)}) copy-start(f32[8,32]{1,0:T(8,128)S(1)} %get-tuple-element.12) | copy-start | bytes 3076
  32.2 69.3 %copy-start.50 = (f32[8]{0:T(128)}, f32[8]{0:T(128)S(1)}, u32[]{:S(2)}) copy-start(f32[8]{0:T(128)S(1)} %get-tuple-element.11) | copy-start | bytes 100
  32.3 69.3 %copy-start.24 = (f32[768]{0:T(1024)}, f32[768]{0:T(1024)S(1)}, u32[]{:S(2)}) copy-start(f32[768]{0:T(1024)S(1)} %get-tuple-element.5) | copy-start | bytes 9220
  32.3 69.3 %copy-start.22 = (f32[768]{0:T(1024)}, f32[768]{0:T(1024)S(1)}, u32[]{:S(2)}) copy-start(f32[768]{0:T(1024)S(1)} %get-tuple-element.6) | copy-start | bytes 9220
  59.6 3.0 copy-start.52
  63.3 109.3 %copy-start.20 = (f32[8,768]{1,0:T(8,128)}, f32[8,768]{1,0:T(8,128)S(1)}, u32[]{:S(2)}) copy-start(f32[8,768]{1,0:T(8,128)S(1)} %get-tuple-element.27) | copy-start | bytes 73732
  63.3 109.3 %copy-start.62 = (f32[8]{0:T(128)}, f32[8]{0:T(128)S(1)}, u32[]{:S(2)}) copy-start(f32[8]{0:T(128)S(1)} %get-tuple-element.26) | copy-start | bytes 100
  63.4 109.3 %copy-start.42 = (f32[8]{0:T(128)}, f32[8]{0:T(128)S(1)}, u32[]{:S(2)}) copy-start(f32[8]{0:T(128)S(1)} %add_rsqrt_fusion.3) | copy-start | bytes 100
  100.0 3.0 copy-start.53
  101.5 71.2 %copy-start.39 = (f32[4,64]{1,0:T(4,128)}, f32[4,64]{1,0:T(4,128)S(1)}, u32[]{:S(2)}) copy-start(f32[4,64]{1,0:T(4,128)S(1)} %multiply_reduce_fusion.3) | copy-start | bytes 3076
  101.6 71.2 %copy-start.37 = (f32[4,64]{1,0:T(4,128)}, f32[4,64]{1,0:T(4,128)S(1)}, u32[]{:S(2)}) copy-start(f32[4,64]{1,0:T(4,128)S(1)} %fusion.94) | copy-start | bytes 3076
  103.8 69.0 %copy-start.48 = (f32[4]{0:T(128)}, f32[4]{0:T(128)S(1)}, u32[]{:S(2)}) copy-start(f32[4]{0:T(128)S(1)} %add_rsqrt_fusion.2) | copy-start | bytes 52
  105.1 240.0 %all-gather.6.cloned.1.call-start = ((), (), s32[]{:S(2)}) async-start(), calls=%async_computation.5 | async-start | bytes 1966080 | tf_op jit(solution)/shard_map/all_gather | solution.py:172
  173.2 3.6 copy-start.10
  181.8 129.7 %copy-start.8 = (s32[1024,16]{1,0:T(8,128)S(1)}, s32[1024,16]{1,0:T(8,128)}, u32[]{:S(2)}) copy-start(s32[1024,16]{1,0:T(8,128)} %get-tuple-element.10) | copy-start | bytes 196612
  311.6 3.9 copy-start.21
  312.0 5.3 %copy-start.63 = (f32[8]{0:T(128)S(1)}, f32[8]{0:T(128)}, u32[]{:S(2)}) copy-start(f32[8]{0:T(128)} %copy-done.62) | copy-start | bytes 100
  312.0 5.3 %copy-start.43 = (f32[8]{0:T(128)S(1)}, f32[8]{0:T(128)}, u32[]{:S(2)}) copy-start(f32[8]{0:T(128)} %copy-done.42) | copy-start | bytes 100
  312.0 5.3 %copy-start.51 = (f32[8]{0:T(128)S(1)}, f32[8]{0:T(128)}, u32[]{:S(2)}) copy-start(f32[8]{0:T(128)} %copy-done.50) | copy-start | bytes 100
  313.6 6.0 %copy-start.3 = (bf16[32,32,768]{2,1,0:T(8,128)(2,1)S(1)}, bf16[32,32,768]{2,1,0:T(8,128)(2,1)}, u32[]{:S(2)}) copy-start(bf16[32,32,768]{2,1,0:T(8,128)(2,1)} %param.13) | copy-start | bytes 4718596
  313.6 6.0 %copy-start.6 = (f32[8,32,768]{2,1,0:T(8,128)S(1)}, f32[8,32,768]{2,1,0:T(8,128)}, u32[]{:S(2)}) copy-start(f32[8,32,768]{2,1,0:T(8,128)} %reduce-scatter.4.cloned.1.call-done) | copy-start | bytes 2359300
  313.6 6.0 %copy-start.25 = (f32[768]{0:T(1024)S(1)}, f32[768]{0:T(1024)}, u32[]{:S(2)}) copy-start(f32[768]{0:T(1024)} %copy-done.24) | copy-start | bytes 9220
  313.6 6.0 %copy-start.27 = (f32[8,32]{1,0:T(8,128)S(1)}, f32[8,32]{1,0:T(8,128)}, u32[]{:S(2)}) copy-start(f32[8,32]{1,0:T(8,128)} %copy-done.26) | copy-start | bytes 3076
  314.7 5.3 %copy-start.34 = (f32[8,32]{1,0:T(8,128)S(1)}, f32[8,32]{1,0:T(8,128)}, u32[]{:S(2)}) copy-start(f32[8,32]{1,0:T(8,128)} %copy-done.33) | copy-start | bytes 3076
  314.7 5.3 %copy-start.32 = (f32[8,32]{1,0:T(8,128)S(1)}, f32[8,32]{1,0:T(8,128)}, u32[]{:S(2)}) copy-start(f32[8,32]{1,0:T(8,128)} %copy-done.31) | copy-start | bytes 3076
  320.0 2.9 copy-start.29
  321.1 51.9 %all-gather.8.cloned.1.call-start = ((), (), s32[]{:S(2)}) async-start(), calls=%async_computation.6 | async-start | bytes 1966080 | tf_op jit(solution)/shard_map/all_gather | solution.py:173
  321.3 4.1 copy-start.61
  321.3 4.1 copy-start.47
  321.3 4.1 copy-start.49
  322.6 5.1 %copy-start.5 = (bf16[16,64,768]{2,1,0:T(8,128)(2,1)S(1)}, bf16[16,64,768]{2,1,0:T(8,128)(2,1)}, u32[]{:S(2)}) copy-start(bf16[16,64,768]{2,1,0:T(8,128)(2,1)} %param.14) | copy-start | bytes 4718596
  322.6 5.1 %copy-start.7 = (f32[4,64,768]{2,1,0:T(8,128)S(1)}, f32[4,64,768]{2,1,0:T(8,128)}, u32[]{:S(2)}) copy-start(f32[4,64,768]{2,1,0:T(8,128)} %reduce-scatter.6.cloned.1.call-done) | copy-start | bytes 2359300
  322.6 5.2 %copy-start.23 = (f32[768]{0:T(1024)S(1)}, f32[768]{0:T(1024)}, u32[]{:S(2)}) copy-start(f32[768]{0:T(1024)} %copy-done.22) | copy-start | bytes 9220
  322.6 5.2 %copy-start.36 = (f32[4,64]{1,0:T(4,128)S(1)}, f32[4,64]{1,0:T(4,128)}, u32[]{:S(2)}) copy-start(f32[4,64]{1,0:T(4,128)} %copy-done.35) | copy-start | bytes 3076
  322.8 5.3 %copy-start.40 = (f32[4,64]{1,0:T(4,128)S(1)}, f32[4,64]{1,0:T(4,128)}, u32[]{:S(2)}) copy-start(f32[4,64]{1,0:T(4,128)} %copy-done.39) | copy-start | bytes 3076
  322.9 5.2 %copy-start.38 = (f32[4,64]{1,0:T(4,128)S(1)}, f32[4,64]{1,0:T(4,128)}, u32[]{:S(2)}) copy-start(f32[4,64]{1,0:T(4,128)} %copy-done.37) | copy-start | bytes 3076
  329.2 158.4 %reduce-scatter.8.cloned.1.call-start = ((), (), s32[]{:S(2)}) async-start(), calls=%async_computation.7 | async-start | bytes 9732096 | tf_op jit(solution)/shard_map/reduce_scatter | solution.py:202
  373.0 3.9 copy-start.66
  391.7 97.6 %copy-start.1 = (s32[32,15]{0,1:T(8,128)S(1)}, s32[32,15]{0,1:T(8,128)}, u32[]{:S(2)}) copy-start(s32[32,15]{0,1:T(8,128)} %param.24) | copy-start | bytes 5764
  (29 other events, 48.4 us)
Sparse Core Ops, SparseCore 0:
  18.8 40.7 reduce-scatter.3
  62.0 37.9 reduce-scatter.5
  105.2 65.5 all-gather.9
  321.2 23.8 all-gather.5
  346.6 26.3 all-gather.7
  391.8 95.7 reduce-scatter.7

commit v4 on v3

--- a/solution.py
+++ b/solution.py
@@ -141,14 +141,16 @@
     all_scores = lax.dot_general(
         query_all, passage_all, (((1,), (1,)), ((), ())), preferred_element_type=jnp.float32
     )
-    scores = jnp.take_along_axis(all_scores, cand_all, axis=1)
+    every_id = lax.broadcasted_iota(jnp.int32, (1, 1, passage_total), 2)
+    scores = jnp.sum(
+        jnp.where(cand_all[:, :, None] == every_id, all_scores[:, None, :], 0.0), axis=2
+    )
     score_grads = score_grads_of(scores, counts_all)
     dp_index = lax.axis_index("dp")
     query_start = (dp_index * segments + segment_index) * query_dev
     passage_start = (dp_index * segments + segment_index) * passage_dev
     own_cand = lax.dynamic_slice_in_dim(cand_all, query_start, query_dev, 0)
     own_grads = lax.dynamic_slice_in_dim(score_grads, query_start, query_dev, 0)
-    every_id = lax.broadcasted_iota(jnp.int32, (1, 1, passage_total), 2)
     query_coef = jnp.sum(
         jnp.where(own_cand[:, :, None] == every_id, own_grads[:, :, None], 0.0), axis=1
     )

time: 497 us -> 379 us (0.76)
  local copies, waits for them, and re-layouts: 150 us -> 24.9 us
  other arithmetic: 25.1 us -> 33.8 us
    gather x3 -> x0, local copies, waits for them, and re-layouts: 130 us -> none  [body(): scores = jnp.take_along_axis(all_scores, cand_all, axis=1)]
    reduce_sum x0 -> x1, other arithmetic: none -> 6.83 us  [body(): jnp.sum(jnp.where(cand_all[:, :, None] == every_id, all_scores[:, None, :...]
  transfers between devices with their start and end apart: 6 -> 6, of which waited for: 6 -> 6; matrix products, arithmetic and copies ran while one was open for 5% -> 7% of each run, Pallas kernels for 0% -> 0%
where the time goes in v4:
time: 379 us; the launch traced here: 378 us
  waiting for transfers between devices  262 us (69%)
  matrix products  42.2 us (11%)
  other arithmetic  33.8 us (9%)
  local copies, waits for them, and re-layouts  24.9 us (7%)
  between operations  14.6 us (4%)
    reduce_scatter x1, waiting for transfers between devices, body(): lax.psum_scatter(weight_terms(), 'dp', scatter_dimension=0, tiled=True)  95.9 us
    all_gather x1, waiting for transfers between devices, body(): gathered = lax.all_gather(packed, ('dp', 'segment'), axis=0, tiled=False)  65.5 us
    reduce_scatter x1, waiting for transfers between devices, body(): lax.psum_scatter(passage_parts[5], 'segment', scatter_dimension=0, tiled=...  36.7 us
    reduce_scatter x1, waiting for transfers between devices, body(): lax.psum_scatter(query_parts[5], 'segment', scatter_dimension=0, tiled=True)  27.4 us
    all_gather x1, waiting for transfers between devices, body(): lax.all_gather(passage_share, 'segment', axis=0, tiled=True)  21.6 us
    all_gather x1, waiting for transfers between devices, body(): lax.all_gather(query_share, 'segment', axis=0, tiled=True)  14.7 us
    dot_general x6, matrix products, contract(): lax.dot_general(left, right, (((0,), (0,)), ((), ())), preferred_element_...  13.6 us
    unnamed x75, local copies, waits for them, and re-layouts  7.99 us
  transfers between devices with their start and end apart: 6, of which 6 were waited for; matrix products, arithmetic and copies ran while one was open for 7% of the time, Pallas kernels for 0%

profile of v4, /device:TPU:0, one launch (start us, length us, event | category | flops | bytes accessed | tf_op | source)
XLA Modules:
  0.0 378.0 jit_solution(17677148004995297710)
XLA Ops:
  8.1 1.9 fusion
  10.5 1.0 fusion.56
  12.5 2.6 multiply_convert_fusion.3
  15.1 1.0 copy-done.16
  16.1 2.6 fusion.50
  18.8 1.3 copy-done.3
  21.5 1.0 fusion.48
  23.0 2.6 multiply_convert_fusion.2
  26.5 2.7 fusion.42
  32.2 27.4 %reduce-scatter.4.cloned.1.call-done = f32[8,32,768]{2,1,0:T(8,128)} async-done(((f32[32,32,768]{2,1,0:T(8,128)}), f32[8,32,768]{2,1,0:T(8,128)}) %reduce-scatter.4.cloned.1.call-update) | async-done | bytes 786448 | tf_op jit(solution)/shard_map/reduce_scatter | solution.py:100
  59.6 1.5 multiply_reduce_fusion.5
  61.1 1.4 multiply_reduce_fusion.4
  63.3 36.7 %reduce-scatter.6.cloned.1.call-done = f32[4,64,768]{2,1,0:T(8,128)} async-done(((f32[16,64,768]{2,1,0:T(8,128)}), f32[4,64,768]{2,1,0:T(8,128)}) %reduce-scatter.6.cloned.1.call-update) | async-done | bytes 786448 | tf_op jit(solution)/shard_map/reduce_scatter | solution.py:101
  100.1 1.5 multiply_reduce_fusion.3
  101.5 1.4 multiply_reduce_fusion.2
  104.7 65.5 %all-gather.10.cloned.1.call-done = bf16[128,13,768]{2,1,0:T(8,128)(2,1)} async-done(((bf16[1,13,768]{2,1,0:T(8,128)(2,1)}), bf16[128,13,768]{2,1,0:T(8,128)(2,1)}) %all-gather.10.cloned.1.call-update) | async-done | bytes 2555920 | tf_op jit(solution)/shard_map/all_gather | solution.py:128
  170.3 1.8 slice.98
  172.3 1.1 reshape.155
  173.4 1.6 slice_reduce_fusion.1
  174.9 2.2 slice_add_fusion
  177.2 2.5 slice.104
  179.7 1.3 slice.103
  181.0 2.3 reshape.152
  183.9 2.7 fusion.121
  186.6 6.8 %select_reduce_fusion = f32[1024,16]{1,0:T(8,128)S(1)} fusion(f32[1024,512]{1,0:T(8,128)S(1)} %fusion.121, s32[1024,16]{1,0:T(8,128)S(1)} %copy-done.6), kind=kLoop, calls=%fused_computation | loop fusion | flops 25149440 | bytes 2228224 | tf_op jit(solution)/shard_map/reduce_sum | solution.py:145
  194.3 1.6 fusion.115
  195.9 1.0 copy.45
  197.9 1.7 multiply_reduce_fusion.6
  199.6 2.3 fusion.28
  202.3 1.0 fusion.40
  203.4 1.2 copy.46
  204.6 1.4 pad_add_fusion
  206.3 2.2 multiply_reduce_fusion.8
  208.6 2.4 fusion.31
  211.3 1.1 fusion.41
  212.6 14.7 %all-gather.6.cloned.1.call-done = bf16[32,32,768]{2,1,0:T(8,128)(2,1)} async-done(((bf16[8,32,768]{2,1,0:T(8,128)(2,1)}), bf16[32,32,768]{2,1,0:T(8,128)(2,1)}) %all-gather.6.cloned.1.call-update) | async-done | bytes 1572880 | tf_op jit(solution)/shard_map/all_gather | solution.py:174
  227.3 4.0 %convolution_bitcast_fusion.1 = f32[768,1,512]{2,0,1:T(8,128)} fusion(bf16[1024,768]{1,0:T(8,128)(2,1)} %bitcast.133, bf16[1024,512]{1,0:T(8,128)(2,1)} %copy-done.16), kind=kOutput, calls=%fused_computation.41 | convolution fusion | flops 805306368 | bytes 4194304 | tf_op jit(solution)/shard_map/dot_general | solution.py:37
  231.3 2.4 fusion.52
  233.7 21.6 %all-gather.8.cloned.1.call-done = bf16[16,64,768]{2,1,0:T(8,128)(2,1)} async-done(((bf16[4,64,768]{2,1,0:T(8,128)(2,1)}), bf16[16,64,768]{2,1,0:T(8,128)(2,1)}) %all-gather.8.cloned.1.call-update) | async-done | bytes 1572880 | tf_op jit(solution)/shard_map/all_gather | solution.py:175
  255.3 2.6 convolution_bitcast_fusion
  257.8 1.0 fusion.44
  259.9 1.1 convolution_bitcast_fusion.3
  261.5 2.4 convolution_bitcast_fusion.5
  263.9 1.1 convolution_bitcast_fusion.2
  265.5 2.4 convolution_bitcast_fusion.4
  268.8 4.7 %pad_maximum_fusion = f32[768,3,2,512]{3,0,2,1:T(8,128)} fusion(f32[768,1,2,512]{3,0,2,1:T(8,128)S(1)} %maximum_bitcast_fusion.2, f32[768,1,2,512]{3,0,2,1:T(8,128)S(1)} %maximum_bitcast_fusion.1, f32[768,1,2,512]{3,0,2,1:T(8,128)S(1)} %maximum_bitcast_fusion), kind=kLoop, calls=%fused_computation.2 | loop fusion | flops 4718592 | bytes 18874368 | tf_op jit(solution)/shard_map/stack | solution.py:202
  273.6 95.9 %reduce-scatter.8.cloned.1.call-done = f32[24,3,2,512]{3,0,2,1:T(8,128)} async-done(((f32[768,3,2,512]{3,0,2,1:T(8,128)}), f32[24,3,2,512]{3,0,2,1:T(8,128)}) %reduce-scatter.8.cloned.1.call-update) | async-done | bytes 294928 | tf_op jit(solution)/shard_map/reduce_scatter | solution.py:204
  369.5 1.7 slice_bitcast_fusion
  (134 shorter events, 17.6 us)
Async XLA Ops:
  7.2 23.0 %copy-start = (s32[32,15]{0,1:T(8,128)S(1)}, s32[32,15]{0,1:T(8,128)}, u32[]{:S(2)}) copy-start(s32[32,15]{0,1:T(8,128)} %param.24) | copy-start | bytes 5764
  7.2 2.8 copy-start.2
  7.2 52.5 %reduce-scatter.4.cloned.1.call-start = ((), (), s32[]{:S(2)}) async-start(), calls=%async_computation.3 | async-start | bytes 3932160 | tf_op jit(solution)/shard_map/reduce_scatter | solution.py:100
  8.1 2.4 copy-start.24
  10.5 1.2 copy-start.11
  10.5 2.0 copy-start.26
  12.5 2.6 copy-start.31
  12.5 3.6 copy-start.8
  15.1 1.0 copy-start.16
  18.7 1.4 copy-start.3
  18.7 81.3 %reduce-scatter.6.cloned.1.call-start = ((), (), s32[]{:S(2)}) async-start(), calls=%async_computation.4 | async-start | bytes 3932160 | tf_op jit(solution)/shard_map/reduce_scatter | solution.py:101
  20.1 1.4 copy-start.25
  21.0 1.6 copy-start.13
  21.5 1.4 copy-start.27
  22.9 2.6 copy-start.33
  22.9 3.6 copy-start.9
  25.5 1.0 copy-start.17
  29.2 0.7 copy-start.20
  29.2 0.7 copy-start.21
  29.2 3.0 copy-start.19
  29.2 141.0 %all-gather.10.cloned.1.call-start = ((), (), s32[]{:S(2)}) async-start(), calls=%async_computation.8 | async-start | bytes 3170304 | tf_op jit(solution)/shard_map/all_gather | solution.py:128
  59.6 2.9 copy-start.22
  100.1 2.9 copy-start.23
  104.5 122.8 %all-gather.6.cloned.1.call-start = ((), (), s32[]{:S(2)}) async-start(), calls=%async_computation.5 | async-start | bytes 1966080 | tf_op jit(solution)/shard_map/all_gather | solution.py:174
  173.4 6.3 %copy-start.7 = (bf16[128,13,768]{2,1,0:T(8,128)(2,1)S(1)}, bf16[128,13,768]{2,1,0:T(8,128)(2,1)}, u32[]{:S(2)}) copy-start(bf16[128,13,768]{2,1,0:T(8,128)(2,1)} %all-gather.10.cloned.1.call-done) | copy-start | bytes 7667716
  183.9 2.7 copy-start.6
  196.9 5.0 %copy-start.4 = (f32[8,32,768]{2,1,0:T(8,128)S(1)}, f32[8,32,768]{2,1,0:T(8,128)}, u32[]{:S(2)}) copy-start(f32[8,32,768]{2,1,0:T(8,128)} %reduce-scatter.4.cloned.1.call-done) | copy-start | bytes 2359300
  203.3 51.9 %all-gather.8.cloned.1.call-start = ((), (), s32[]{:S(2)}) async-start(), calls=%async_computation.6 | async-start | bytes 1966080 | tf_op jit(solution)/shard_map/all_gather | solution.py:175
  206.0 4.9 %copy-start.5 = (f32[4,64,768]{2,1,0:T(8,128)S(1)}, f32[4,64,768]{2,1,0:T(8,128)}, u32[]{:S(2)}) copy-start(f32[4,64,768]{2,1,0:T(8,128)} %reduce-scatter.6.cloned.1.call-done) | copy-start | bytes 2359300
  212.4 157.1 %reduce-scatter.8.cloned.1.call-start = ((), (), s32[]{:S(2)}) async-start(), calls=%async_computation.7 | async-start | bytes 9732096 | tf_op jit(solution)/shard_map/reduce_scatter | solution.py:204
  227.3 4.0 %copy-start.10 = (bf16[2,512,768]{2,1,0:T(8,128)(2,1)S(1)}, bf16[2,512,768]{2,1,0:T(8,128)(2,1)}, u32[]{:S(2)}) copy-start(bf16[2,512,768]{2,1,0:T(8,128)(2,1)} %param.21) | copy-start | bytes 4718596
  227.3 4.0 %copy-start.28 = (bf16[32,32,768]{2,1,0:T(8,128)(2,1)S(1)}, bf16[32,32,768]{2,1,0:T(8,128)(2,1)}, u32[]{:S(2)}) copy-start(bf16[32,32,768]{2,1,0:T(8,128)(2,1)} %all-gather.6.cloned.1.call-done) | copy-start | bytes 4718596
  231.3 23.9 %copy-start.18 = (bf16[1024,512]{1,0:T(8,128)(2,1)S(1)}, bf16[1024,512]{1,0:T(8,128)(2,1)}, u32[]{:S(2)}) copy-start(bf16[1024,512]{1,0:T(8,128)(2,1)} %copy-done.17) | copy-start | bytes 3145732
  255.2 2.6 copy-start.29
  255.3 3.6 copy-start.32
  257.8 1.4 copy-start.12
  257.8 2.1 copy-start.30
  259.9 1.6 copy-start.35
  261.5 2.4 copy-start.14
  261.5 2.4 copy-start.34
  263.9 1.6 copy-start.36
  265.5 2.4 copy-start.15
  273.6 97.6 %copy-start.1 = (s32[32,15]{0,1:T(8,128)S(1)}, s32[32,15]{0,1:T(8,128)}, u32[]{:S(2)}) copy-start(s32[32,15]{0,1:T(8,128)} %param.24) | copy-start | bytes 5764
Sparse Core Ops, SparseCore 0:
  18.9 40.7 reduce-scatter.3
  62.1 37.9 reduce-scatter.5
  104.6 65.5 all-gather.9
  203.4 23.8 all-gather.5
  228.8 26.4 all-gather.7
  273.7 95.7 reduce-scatter.7

commit v5 on v4

--- a/solution.py
+++ b/solution.py
@@ -201,7 +201,9 @@
             matrices[2].append(contract(flat_grad, hidden))
         return jnp.stack([jnp.stack(pieces, axis=1) for pieces in matrices], axis=1)
 
-    summed_grads = lax.psum_scatter(weight_terms(), "dp", scatter_dimension=0, tiled=True)
+    summed_grads = lax.psum_scatter(
+        weight_terms().astype(jnp.bfloat16), "dp", scatter_dimension=0, tiled=True
+    ).astype(jnp.float32)
     grad_gate = jnp.transpose(summed_grads[:, 0], (1, 0, 2))
     grad_up = jnp.transpose(summed_grads[:, 1], (1, 0, 2))
     grad_down = jnp.transpose(summed_grads[:, 2], (1, 2, 0))

time: 379 us -> 385 us (1.016)
  local copies, waits for them, and re-layouts: 24.9 us -> 46 us
  waiting for transfers between devices: 262 us -> 251 us
    reduce_scatter x1 -> x0, waiting for transfers between devices: 95.9 us -> none  [body(): lax.psum_scatter(weight_terms(), 'dp', scatter_dimension=0, tiled=True)]
    unnamed x6 -> x7, waiting for transfers between devices: 0.1 us -> 84.4 us
    unnamed x75 -> x78, local copies, waits for them, and re-layouts: 7.99 us -> 30.1 us
where the time goes in v5:
time: 385 us; the launch traced here: 384 us
  waiting for transfers between devices  251 us (65%)
  local copies, waits for them, and re-layouts  46 us (12%)
  matrix products  41 us (11%)
  other arithmetic  31.3 us (8%)
  between operations  14.6 us (4%)
    unnamed x7, waiting for transfers between devices  84.4 us
    all_gather x1, waiting for transfers between devices, body(): gathered = lax.all_gather(packed, ('dp', 'segment'), axis=0, tiled=False)  65.5 us
    reduce_scatter x1, waiting for transfers between devices, body(): lax.psum_scatter(passage_parts[5], 'segment', scatter_dimension=0, tiled=...  36.7 us
    unnamed x78, local copies, waits for them, and re-layouts  30.1 us
    reduce_scatter x1, waiting for transfers between devices, body(): lax.psum_scatter(query_parts[5], 'segment', scatter_dimension=0, tiled=True)  27.4 us
    all_gather x1, waiting for transfers between devices, body(): lax.all_gather(passage_share, 'segment', axis=0, tiled=True)  21.9 us
    all_gather x1, waiting for transfers between devices, body(): lax.all_gather(query_share, 'segment', axis=0, tiled=True)  14.6 us
    dot_general x6, matrix products, contract(): lax.dot_general(left, right, (((0,), (0,)), ((), ())), preferred_element_...  12.4 us
  transfers between devices with their start and end apart: 6, of which 6 were waited for; matrix products, arithmetic and copies ran while one was open for 7% of the time, Pallas kernels for 0%

profile of v5, /device:TPU:0, one launch (start us, length us, event | category | flops | bytes accessed | tf_op | source)
XLA Modules:
  0.0 384.2 jit_solution(11809702654739627732)
XLA Ops:
  8.1 1.9 fusion
  12.5 2.6 multiply_convert_fusion.3
  15.1 1.0 copy-done.15
  16.1 2.6 fusion.56
  18.8 1.3 copy-done.3
  23.0 2.6 multiply_convert_fusion.2
  26.6 2.7 fusion.48
  32.3 27.4 %reduce-scatter.6.cloned.1.call-done = f32[8,32,768]{2,1,0:T(8,128)} async-done(((f32[32,32,768]{2,1,0:T(8,128)}), f32[8,32,768]{2,1,0:T(8,128)}) %reduce-scatter.6.cloned.1.call-update) | async-done | bytes 786448 | tf_op jit(solution)/shard_map/reduce_scatter | solution.py:100
  59.7 1.5 multiply_reduce_fusion.5
  61.2 1.4 multiply_reduce_fusion.4
  63.4 36.7 %reduce-scatter.8.cloned.1.call-done = f32[4,64,768]{2,1,0:T(8,128)} async-done(((f32[16,64,768]{2,1,0:T(8,128)}), f32[4,64,768]{2,1,0:T(8,128)}) %reduce-scatter.8.cloned.1.call-update) | async-done | bytes 786448 | tf_op jit(solution)/shard_map/reduce_scatter | solution.py:101
  100.1 1.5 multiply_reduce_fusion.3
  101.6 1.4 multiply_reduce_fusion.2
  104.8 65.5 %all-gather.10.cloned.1.call-done = bf16[128,13,768]{2,1,0:T(8,128)(2,1)} async-done(((bf16[1,13,768]{2,1,0:T(8,128)(2,1)}), bf16[128,13,768]{2,1,0:T(8,128)(2,1)}) %all-gather.10.cloned.1.call-update) | async-done | bytes 2555920 | tf_op jit(solution)/shard_map/all_gather | solution.py:128
  170.3 1.8 slice.98
  172.3 1.0 reshape.155
  173.4 1.6 slice_reduce_fusion.1
  174.9 2.2 slice_add_fusion
  177.1 2.5 slice.104
  179.6 1.3 slice.103
  180.9 2.3 reshape.152
  183.9 2.7 fusion.127
  186.6 6.8 %select_reduce_fusion = f32[1024,16]{1,0:T(8,128)S(1)} fusion(f32[1024,512]{1,0:T(8,128)S(1)} %fusion.127, s32[1024,16]{1,0:T(8,128)S(1)} %copy-done.6), kind=kLoop, calls=%fused_computation | loop fusion | flops 25149440 | bytes 2228224 | tf_op jit(solution)/shard_map/reduce_sum | solution.py:145
  194.3 1.6 fusion.121
  195.8 1.0 copy.45
  197.9 1.7 multiply_reduce_fusion.6
  199.5 2.3 fusion.34
  202.2 1.0 fusion.46
  203.3 1.2 copy.46
  204.5 1.4 pad_add_fusion
  206.3 2.2 multiply_reduce_fusion.8
  208.5 2.4 fusion.37
  211.2 1.1 fusion.47
  212.6 14.6 %all-gather.6.cloned.1.call-done = bf16[32,32,768]{2,1,0:T(8,128)(2,1)} async-done(((bf16[8,32,768]{2,1,0:T(8,128)(2,1)}), bf16[32,32,768]{2,1,0:T(8,128)(2,1)}) %all-gather.6.cloned.1.call-update) | async-done | bytes 1572880 | tf_op jit(solution)/shard_map/all_gather | solution.py:174
  227.3 3.7 fusion.24
  231.0 2.4 fusion.58
  233.4 21.9 %all-gather.8.cloned.1.call-done = bf16[16,64,768]{2,1,0:T(8,128)(2,1)} async-done(((bf16[4,64,768]{2,1,0:T(8,128)(2,1)}), bf16[16,64,768]{2,1,0:T(8,128)(2,1)}) %all-gather.8.cloned.1.call-update) | async-done | bytes 1572880 | tf_op jit(solution)/shard_map/all_gather | solution.py:175
  255.3 2.6 fusion.25
  257.9 1.0 fusion.50
  259.9 1.1 fusion.22
  261.5 1.9 fusion.20
  263.6 1.1 fusion.23
  265.2 1.9 fusion.21
  267.6 2.7 pad_maximum_fusion
  270.3 9.3 %copy.49 = bf16[768,3,2,512]{3,2,1,0:T(2,128)(2,1)} copy(bf16[768,3,2,512]{3,0,2,1:T(8,128)(2,1)} %pad_maximum_fusion) | data formatting | bytes 9437184
  279.6 11.6 %reshape.163 = bf16[768,3072]{1,0:T(8,128)(2,1)} reshape(bf16[768,3,2,512]{3,2,1,0:T(2,128)(2,1)} %copy.49) | data formatting | bytes 9437184
  291.2 84.4 %reduce-scatter.10.cloned.1.call-done = bf16[24,3072]{1,0:T(8,128)(2,1)} async-done(((bf16[768,3072]{1,0:T(8,128)(2,1)}), bf16[24,3072]{1,0:T(8,128)(2,1)}) %reduce-scatter.10.cloned.1.call-update) | async-done | bytes 147472
  375.6 1.0 reshape.164
  (138 shorter events, 20.0 us)
Async XLA Ops:
  7.2 23.0 %copy-start = (s32[32,15]{0,1:T(8,128)S(1)}, s32[32,15]{0,1:T(8,128)}, u32[]{:S(2)}) copy-start(s32[32,15]{0,1:T(8,128)} %param.24) | copy-start | bytes 5764
  7.2 2.8 copy-start.2
  7.2 52.5 %reduce-scatter.6.cloned.1.call-start = ((), (), s32[]{:S(2)}) async-start(), calls=%async_computation.3 | async-start | bytes 3932160 | tf_op jit(solution)/shard_map/reduce_scatter | solution.py:100
  8.1 2.4 copy-start.24
  10.5 1.2 copy-start.11
  10.5 2.0 copy-start.26
  12.5 2.6 copy-start.31
  12.5 3.7 copy-start.8
  15.1 1.0 copy-start.15
  18.8 1.4 copy-start.3
  18.8 81.3 %reduce-scatter.8.cloned.1.call-start = ((), (), s32[]{:S(2)}) async-start(), calls=%async_computation.4 | async-start | bytes 3932160 | tf_op jit(solution)/shard_map/reduce_scatter | solution.py:101
  20.2 1.4 copy-start.25
  21.0 1.6 copy-start.13
  21.6 1.4 copy-start.27
  23.0 2.6 copy-start.33
  23.0 3.6 copy-start.9
  25.6 1.0 copy-start.16
  29.2 0.7 copy-start.20
  29.2 0.7 copy-start.21
  29.2 3.0 copy-start.19
  29.3 141.0 %all-gather.10.cloned.1.call-start = ((), (), s32[]{:S(2)}) async-start(), calls=%async_computation.7 | async-start | bytes 3170304 | tf_op jit(solution)/shard_map/all_gather | solution.py:128
  59.7 2.9 copy-start.22
  100.1 2.9 copy-start.23
  104.5 122.7 %all-gather.6.cloned.1.call-start = ((), (), s32[]{:S(2)}) async-start(), calls=%async_computation.5 | async-start | bytes 1966080 | tf_op jit(solution)/shard_map/all_gather | solution.py:174
  173.4 6.3 %copy-start.7 = (bf16[128,13,768]{2,1,0:T(8,128)(2,1)S(1)}, bf16[128,13,768]{2,1,0:T(8,128)(2,1)}, u32[]{:S(2)}) copy-start(bf16[128,13,768]{2,1,0:T(8,128)(2,1)} %all-gather.10.cloned.1.call-done) | copy-start | bytes 7667716
  183.9 2.7 copy-start.6
  196.9 5.0 %copy-start.4 = (f32[8,32,768]{2,1,0:T(8,128)S(1)}, f32[8,32,768]{2,1,0:T(8,128)}, u32[]{:S(2)}) copy-start(f32[8,32,768]{2,1,0:T(8,128)} %reduce-scatter.6.cloned.1.call-done) | copy-start | bytes 2359300
  203.3 52.0 %all-gather.8.cloned.1.call-start = ((), (), s32[]{:S(2)}) async-start(), calls=%async_computation.6 | async-start | bytes 1966080 | tf_op jit(solution)/shard_map/all_gather | solution.py:175
  206.0 4.9 %copy-start.5 = (f32[4,64,768]{2,1,0:T(8,128)S(1)}, f32[4,64,768]{2,1,0:T(8,128)}, u32[]{:S(2)}) copy-start(f32[4,64,768]{2,1,0:T(8,128)} %reduce-scatter.8.cloned.1.call-done) | copy-start | bytes 2359300
  212.3 163.2 %reduce-scatter.10.cloned.1.call-start = ((), (), s32[]{:S(2)}) async-start(), calls=%async_computation.8 | async-start | bytes 4866048
  227.3 3.8 copy-start.10
  227.3 3.8 copy-start.28
  231.0 24.3 %copy-start.17 = (bf16[1024,512]{1,0:T(8,128)(2,1)S(1)}, bf16[1024,512]{1,0:T(8,128)(2,1)}, u32[]{:S(2)}) copy-start(bf16[1024,512]{1,0:T(8,128)(2,1)} %copy-done.16) | copy-start | bytes 3145732
  255.3 2.6 copy-start.29
  255.3 3.6 copy-start.32
  257.9 1.4 copy-start.12
  257.9 2.1 copy-start.30
  259.9 1.6 copy-start.35
  261.5 1.9 copy-start.14
  261.5 2.1 copy-start.34
  263.6 1.6 copy-start.36
  265.2 1.9 copy-start.18
  291.2 86.1 %copy-start.1 = (s32[32,15]{0,1:T(8,128)S(1)}, s32[32,15]{0,1:T(8,128)}, u32[]{:S(2)}) copy-start(s32[32,15]{0,1:T(8,128)} %param.24) | copy-start | bytes 5764
Sparse Core Ops, SparseCore 0:
  18.9 40.7 reduce-scatter.5
  62.1 37.9 reduce-scatter.7
  104.7 65.5 all-gather.9
  203.4 23.8 all-gather.5
  228.8 26.4 all-gather.7
  291.4 84.1 reduce-scatter.9

commit v6 on v4

--- a/solution.py
+++ b/solution.py
@@ -96,10 +96,17 @@
 
     query_parts = forward_part(query_states, 0)
     passage_parts = forward_part(passage_states, 1)
-    query_branch, passage_branch = (
-        lax.psum_scatter(query_parts[5], "segment", scatter_dimension=0, tiled=True),
-        lax.psum_scatter(passage_parts[5], "segment", scatter_dimension=0, tiled=True),
-    )
+    query_block = query_parts[5].reshape(segments, -1, model_width)
+    passage_block = passage_parts[5].reshape(segments, -1, model_width)
+    query_size = query_block.shape[1]
+    branch_sum = lax.psum_scatter(
+        jnp.concatenate([query_block, passage_block], axis=1),
+        "segment",
+        scatter_dimension=0,
+        tiled=True,
+    )[0]
+    query_branch = branch_sum[:query_size].reshape((query_dev,) + query_states.shape[1:])
+    passage_branch = branch_sum[query_size:].reshape((passage_dev,) + passage_states.shape[1:])
     query_embed, query_back = jax.vjp(
         head_of(own_rows(query_tokens, query_dev), 0),
         own_rows(query_states, query_dev).astype(jnp.float32) + query_branch,
@@ -170,10 +177,16 @@
     )
     query_share = query_back(query_grad)[0].astype(jnp.bfloat16)
     passage_share = passage_back(passage_grad)[0].astype(jnp.bfloat16)
-    query_rows, passage_rows = (
-        lax.all_gather(query_share, "segment", axis=0, tiled=True),
-        lax.all_gather(passage_share, "segment", axis=0, tiled=True),
-    )
+    share_rows = lax.all_gather(
+        jnp.concatenate(
+            [query_share.reshape(-1, model_width), passage_share.reshape(-1, model_width)], axis=0
+        ),
+        "segment",
+        axis=0,
+        tiled=False,
+    )
+    query_rows = share_rows[:, :query_size].reshape(query_states.shape)
+    passage_rows = share_rows[:, query_size:].reshape(passage_states.shape)
 
     def backward_part(tower_parts, row_grads, tower_index):
         normed, up_pre, activated, gelu_back, hidden, branch = tower_parts

time: 379 us -> 378 us (level)
  matrix products: 42.2 us -> 33 us
  local copies, waits for them, and re-layouts: 24.9 us -> 29.8 us
    dot_general x6, matrix products: 13.6 us -> 9.07 us  [contract(): lax.dot_general(left, right, (((0,), (0,)), ((), ())), preferred_element_...]
    concatenate x0 -> x2, other arithmetic: none -> 4.07 us  [the longest x1 3.13 us: body(): jnp.concatenate([query_block, passage_block], axis=1)]
    slice x0 -> x2, local copies, waits for them, and re-layouts: none -> 3.83 us  [the longest x1 2.21 us: body(): query_rows = share_rows[:, :query_size].reshape(query_states.shape)]
    unnamed x75 -> x79, local copies, waits for them, and re-layouts: 7.99 us -> 6.11 us
    reduce_scatter x2 -> x1, waiting for transfers between devices: 64.2 us -> 65.2 us  [body(): lax.psum_scatter(jnp.concatenate([query_block, passage_block], axis=1), '...]
    all_gather x2 -> x1, waiting for transfers between devices: 36.2 us -> 36.7 us  [body(): lax.all_gather(jnp.concatenate([query_share.reshape(-1, model_width), pas...]
  transfers between devices with their start and end apart: 6 -> 4, of which waited for: 6 -> 4; matrix products, arithmetic and copies ran while one was open for 7% -> 0% of each run, Pallas kernels for 0% -> 0%
where the time goes in v6:
time: 378 us; the launch traced here: 376 us
  waiting for transfers between devices  263 us (70%)
  other arithmetic  35.7 us (9%)
  matrix products  33 us (9%)
  local copies, waits for them, and re-layouts  29.8 us (8%)
  between operations  14.4 us (4%)
    reduce_scatter x1, waiting for transfers between devices, body(): lax.psum_scatter(weight_terms(), 'dp', scatter_dimension=0, tiled=True)  96.1 us
    reduce_scatter x1, waiting for transfers between devices, body(): lax.psum_scatter(jnp.concatenate([query_block, passage_block], axis=1), '...  65.2 us
    all_gather x1, waiting for transfers between devices, body(): gathered = lax.all_gather(packed, ('dp', 'segment'), axis=0, tiled=False)  64.9 us
    all_gather x1, waiting for transfers between devices, body(): lax.all_gather(jnp.concatenate([query_share.reshape(-1, model_width), pas...  36.7 us
    dot_general x6, matrix products, contract(): lax.dot_general(left, right, (((0,), (0,)), ((), ())), preferred_element_...  9.07 us
  transfers between devices with their start and end apart: 4, of which 4 were waited for; matrix products, arithmetic and copies ran while one was open for 0% of the time, Pallas kernels for 0%

profile of v6, /device:TPU:0, one launch (start us, length us, event | category | flops | bytes accessed | tf_op | source)
XLA Modules:
  0.0 376.5 jit_solution(8314333062079576439)
XLA Ops:
  8.1 1.8 fusion
  9.9 1.9 fusion.3
  12.3 1.0 fusion.56
  13.3 1.1 copy-done.3
  14.8 1.0 fusion.48
  15.8 1.0 copy-done.31
  16.8 2.6 multiply_convert_fusion.3
  19.4 2.7 multiply_convert_fusion.2
  22.1 1.0 fusion.50
  23.1 1.0 fusion.42
  24.1 3.1 pad_maximum_fusion.1
  28.6 65.2 %reduce-scatter.3.cloned.1.call-done = f32[1,512,768]{2,1,0:T(8,128)} async-done(((f32[4,512,768]{2,1,0:T(8,128)}), f32[1,512,768]{2,1,0:T(8,128)}) %reduce-scatter.3.cloned.1.call-update) | async-done | bytes 1572880 | tf_op jit(solution)/shard_map/reduce_scatter | solution.py:102
  93.9 1.6 fusion.122
  95.7 0.9 fusion.117
  102.0 64.9 %all-gather.8.cloned.1.call-done = bf16[128,13,768]{2,1,0:T(8,128)(2,1)} async-done(((bf16[1,13,768]{2,1,0:T(8,128)(2,1)}), bf16[128,13,768]{2,1,0:T(8,128)(2,1)}) %all-gather.8.cloned.1.call-update) | async-done | bytes 2555920 | tf_op jit(solution)/shard_map/all_gather | solution.py:135
  166.9 2.7 slice.123
  169.6 2.5 slice.124
  172.1 1.8 slice.118
  174.2 1.0 reshape.165
  175.2 2.3 slice_add_fusion
  177.5 1.4 slice_reduce_fusion.1
  178.9 2.3 reshape.162
  181.2 2.7 fusion.123
  183.8 6.8 %select_reduce_fusion = f32[1024,16]{1,0:T(8,128)S(1)} fusion(f32[1024,512]{1,0:T(8,128)S(1)} %fusion.123, s32[1024,16]{1,0:T(8,128)S(1)} %copy-done.6), kind=kLoop, calls=%fused_computation | loop fusion | flops 25149440 | bytes 2228224 | tf_op jit(solution)/shard_map/reduce_sum | solution.py:152
  191.5 1.6 fusion.115
  193.1 1.0 copy.45
  195.6 2.2 pad_add_fusion
  197.8 1.8 copy.46
  199.7 1.7 multiply_reduce_fusion.6
  201.4 2.3 fusion.28
  204.4 1.3 copy.47
  205.7 1.0 select_reduce_fusion.2
  206.7 2.2 multiply_reduce_fusion.8
  209.6 2.3 fusion.31
  212.6 0.9 pad_maximum_fusion.2
  213.8 36.7 %all-gather.6.cloned.1.call-done = bf16[2048,768]{1,0:T(8,128)(2,1)} async-done(((bf16[512,768]{1,0:T(8,128)(2,1)}), bf16[2048,768]{1,0:T(8,128)(2,1)}) %all-gather.6.cloned.1.call-update) | async-done | bytes 3145744 | tf_op jit(solution)/shard_map/all_gather | solution.py:180
  250.5 2.2 fusion.121
  252.9 1.0 fusion.52
  254.1 1.0 convolution_bitcast_fusion.1
  255.1 1.0 fusion.44
  256.4 1.0 convolution_bitcast_fusion
  258.4 1.2 convolution_bitcast_fusion.3
  260.0 2.4 convolution_bitcast_fusion.5
  262.5 1.1 convolution_bitcast_fusion.2
  264.0 2.4 convolution_bitcast_fusion.4
  267.4 4.7 %pad_maximum_fusion = f32[768,3,2,512]{3,0,2,1:T(8,128)} fusion(f32[768,1,2,512]{3,0,2,1:T(8,128)S(1)} %maximum_bitcast_fusion.2, f32[768,1,2,512]{3,0,2,1:T(8,128)S(1)} %maximum_bitcast_fusion.1, f32[768,1,2,512]{3,0,2,1:T(8,128)S(1)} %maximum_bitcast_fusion), kind=kLoop, calls=%fused_computation.2 | loop fusion | flops 4718592 | bytes 18874368 | tf_op jit(solution)/shard_map/stack | solution.py:215
  272.1 96.1 %reduce-scatter.5.cloned.1.call-done = f32[24,3,2,512]{3,0,2,1:T(8,128)} async-done(((f32[768,3,2,512]{3,0,2,1:T(8,128)}), f32[24,3,2,512]{3,0,2,1:T(8,128)}) %reduce-scatter.5.cloned.1.call-update) | async-done | bytes 294928 | tf_op jit(solution)/shard_map/reduce_scatter | solution.py:217
  368.2 1.7 slice_bitcast_fusion
  (134 shorter events, 16.9 us)
Async XLA Ops:
  7.2 20.9 %copy-start = (s32[32,15]{0,1:T(8,128)S(1)}, s32[32,15]{0,1:T(8,128)}, u32[]{:S(2)}) copy-start(s32[32,15]{0,1:T(8,128)} %param.24) | copy-start | bytes 5764
  7.2 4.6 %copy-start.2 = (bf16[32,32,768]{2,1,0:T(8,128)(2,1)S(1)}, bf16[32,32,768]{2,1,0:T(8,128)(2,1)}, u32[]{:S(2)}) copy-start(bf16[32,32,768]{2,1,0:T(8,128)(2,1)} %param.13) | copy-start | bytes 4718596
  7.2 86.7 %reduce-scatter.3.cloned.1.call-start = ((), (), s32[]{:S(2)}) async-start(), calls=%async_computation.2 | async-start | bytes 7864320 | tf_op jit(solution)/shard_map/reduce_scatter | solution.py:102
  9.9 2.4 copy-start.30
  12.3 3.5 copy-start.11
  12.3 2.1 copy-start.3
  13.3 2.5 copy-start.35
  14.8 4.6 %copy-start.9 = (bf16[16,64,768]{2,1,0:T(8,128)(2,1)}, bf16[16,64,768]{2,1,0:T(8,128)(2,1)S(1)}, u32[]{:S(2)}) copy-start(bf16[16,64,768]{2,1,0:T(8,128)(2,1)S(1)} %fusion.5) | copy-start | bytes 4718596
  14.8 2.0 copy-start.31
  16.8 2.6 copy-start.33
  19.4 2.7 copy-start.15
  19.4 2.7 copy-start.7
  22.1 1.1 copy-start.13
  27.2 0.7 copy-start.25
  27.2 0.7 copy-start.26
  27.2 1.4 copy-start.24
  27.3 139.7 %all-gather.8.cloned.1.call-start = ((), (), s32[]{:S(2)}) async-start(), calls=%async_computation.5 | async-start | bytes 3170304 | tf_op jit(solution)/shard_map/all_gather | solution.py:135
  93.9 3.0 copy-start.29
  95.5 2.2 copy-start.4
  97.9 1.1 copy-start.22
  98.7 0.6 copy-start.18
  98.7 0.6 copy-start.20
  98.7 1.4 copy-start.27
  100.0 0.5 copy-start.32
  100.0 72.1 %copy-start.17 = (f32[4,768]{1,0:T(4,128)}, f32[4,768]{1,0:T(4,128)S(1)}, u32[]{:S(2)}) copy-start(f32[4,768]{1,0:T(4,128)S(1)} %get-tuple-element.27) | copy-start | bytes 36868
  100.0 72.1 %copy-start.28 = (f32[4]{0:T(128)}, f32[4]{0:T(128)S(1)}, u32[]{:S(2)}) copy-start(f32[4]{0:T(128)S(1)} %add_rsqrt_fusion.2) | copy-start | bytes 52
  101.2 149.3 %all-gather.6.cloned.1.call-start = ((), (), s32[]{:S(2)}) async-start(), calls=%async_computation.4 | async-start | bytes 3932160 | tf_op jit(solution)/shard_map/all_gather | solution.py:180
  181.2 2.7 copy-start.6
  204.4 7.5 %copy-start.5 = (bf16[16,64,768]{2,1,0:T(8,128)(2,1)S(1)}, bf16[16,64,768]{2,1,0:T(8,128)(2,1)}, u32[]{:S(2)}) copy-start(bf16[16,64,768]{2,1,0:T(8,128)(2,1)} %param.14) | copy-start | bytes 4718596
  204.4 7.5 %copy-start.19 = (f32[4,64]{1,0:T(4,128)S(1)}, f32[4,64]{1,0:T(4,128)}, u32[]{:S(2)}) copy-start(f32[4,64]{1,0:T(4,128)} %copy-done.18) | copy-start | bytes 3076
  205.7 6.5 %copy-start.23 = (f32[4,64]{1,0:T(4,128)S(1)}, f32[4,64]{1,0:T(4,128)}, u32[]{:S(2)}) copy-start(f32[4,64]{1,0:T(4,128)} %copy-done.22) | copy-start | bytes 3076
  206.7 5.5 %copy-start.21 = (f32[4,64]{1,0:T(4,128)S(1)}, f32[4,64]{1,0:T(4,128)}, u32[]{:S(2)}) copy-start(f32[4,64]{1,0:T(4,128)} %copy-done.20) | copy-start | bytes 3076
  213.5 154.7 %reduce-scatter.5.cloned.1.call-start = ((), (), s32[]{:S(2)}) async-start(), calls=%async_computation.3 | async-start | bytes 9732096 | tf_op jit(solution)/shard_map/reduce_scatter | solution.py:217
  250.5 2.4 copy-start.8
  252.9 1.2 copy-start.16
  255.1 1.2 copy-start.14
  256.4 1.4 copy-start.12
  256.4 2.1 copy-start.36
  258.4 1.6 copy-start.38
  260.0 2.4 copy-start.10
  260.0 2.4 copy-start.34
  262.4 1.6 copy-start.37
  272.1 97.8 %copy-start.1 = (s32[32,15]{0,1:T(8,128)S(1)}, s32[32,15]{0,1:T(8,128)}, u32[]{:S(2)}) copy-start(s32[32,15]{0,1:T(8,128)} %param.24) | copy-start | bytes 5764
Sparse Core Ops, SparseCore 0:
  27.4 66.4 reduce-scatter.2
  101.3 65.5 all-gather.7
  213.7 36.8 all-gather.5
  272.2 95.9 reduce-scatter.4

commit v7 on v6

--- a/solution.py
+++ b/solution.py
@@ -132,17 +132,21 @@
         own_meta.reshape(-1), (0, meta_rows * model_width - query_dev * meta_width)
     ).reshape(meta_rows, model_width)
     packed = jnp.concatenate([query_round, passage_round, meta_flat], axis=0)
-    gathered = lax.all_gather(packed, ("dp", "segment"), axis=0, tiled=False)
-    gathered = gathered.reshape(groups, segments, -1, model_width)
-    query_all = gathered[:, :, :query_dev].reshape(-1, model_width)
-    passage_all = gathered[:, :, query_dev : query_dev + passage_dev].reshape(-1, model_width)
+    devices = groups * segments
+    gathered = lax.all_gather(packed[:, None, :], ("dp", "segment"), axis=1, tiled=True)
+    query_all = gathered[:query_dev].reshape(-1, model_width)
+    passage_all = gathered[query_dev : query_dev + passage_dev].reshape(-1, model_width)
     meta_all = (
-        gathered[:, :, query_dev + passage_dev :]
-        .reshape(groups, segments, -1)[:, :, : query_dev * meta_width]
+        gathered[query_dev + passage_dev :]
+        .transpose(1, 0, 2)
+        .reshape(devices, -1)[:, : query_dev * meta_width]
+        .reshape(devices, query_dev, meta_width)
+        .transpose(1, 0, 2)
         .reshape(-1, meta_width)
         .astype(jnp.int32)
     )
-    cand_all = meta_all[:, :slots] * id_radix + meta_all[:, slots : 2 * slots]
+    cand_ids = meta_all[:, :slots] * id_radix + meta_all[:, slots : 2 * slots]
+    cand_all = (cand_ids % passage_dev) * devices + cand_ids // passage_dev
     counts_all = meta_all[:, 2 * slots]
     passage_total = passage_all.shape[0]
     all_scores = lax.dot_general(
@@ -153,15 +157,19 @@
         jnp.where(cand_all[:, :, None] == every_id, all_scores[:, None, :], 0.0), axis=2
     )
     score_grads = score_grads_of(scores, counts_all)
-    dp_index = lax.axis_index("dp")
-    query_start = (dp_index * segments + segment_index) * query_dev
-    passage_start = (dp_index * segments + segment_index) * passage_dev
-    own_cand = lax.dynamic_slice_in_dim(cand_all, query_start, query_dev, 0)
-    own_grads = lax.dynamic_slice_in_dim(score_grads, query_start, query_dev, 0)
+    device_index = lax.axis_index("dp") * segments + segment_index
+    own_cand = lax.dynamic_index_in_dim(
+        cand_all.reshape(query_dev, devices, slots), device_index, 1, keepdims=False
+    )
+    own_grads = lax.dynamic_index_in_dim(
+        score_grads.reshape(query_dev, devices, slots), device_index, 1, keepdims=False
+    )
     query_coef = jnp.sum(
         jnp.where(own_cand[:, :, None] == every_id, own_grads[:, :, None], 0.0), axis=1
     )
-    own_passages = passage_start + lax.broadcasted_iota(jnp.int32, (1, 1, passage_dev), 2)
+    own_passages = (
+        lax.broadcasted_iota(jnp.int32, (1, 1, passage_dev), 2) * devices + device_index
+    )
     passage_coef = jnp.sum(
         jnp.where(cand_all[:, :, None] == own_passages, score_grads[:, :, None], 0.0), axis=1
     )

time: 378 us -> 369 us (0.976)
  other arithmetic: 35.7 us -> 27.8 us
    unnamed x79 -> x113, local copies, waits for them, and re-layouts: 6.11 us -> 7.67 us
where the time goes in v7:
time: 369 us; the launch traced here: 368 us
  waiting for transfers between devices  263 us (71%)
  local copies, waits for them, and re-layouts  31.2 us (8%)
  matrix products  30.3 us (8%)
  other arithmetic  27.8 us (8%)
  between operations  14.7 us (4%)
    reduce_scatter x1, waiting for transfers between devices, body(): lax.psum_scatter(weight_terms(), 'dp', scatter_dimension=0, tiled=True)  96.1 us
    reduce_scatter x1, waiting for transfers between devices, body(): lax.psum_scatter(jnp.concatenate([query_block, passage_block], axis=1), '...  65.2 us
    all_gather x1, waiting for transfers between devices, body(): lax.all_gather(packed[:, None, :], ('dp', 'segment'), axis=1, tiled=True)  65 us
    all_gather x1, waiting for transfers between devices, body(): lax.all_gather(jnp.concatenate([query_share.reshape(-1, model_width), pas...  36.9 us
    dot_general x6, matrix products, contract(): lax.dot_general(left, right, (((0,), (0,)), ((), ())), preferred_element_...  9.07 us
    unnamed x113, local copies, waits for them, and re-layouts  7.67 us
  transfers between devices with their start and end apart: 4, of which 4 were waited for; matrix products, arithmetic and copies ran while one was open for 0% of the time, Pallas kernels for 0%

profile of v7, /device:TPU:0, one launch (start us, length us, event | category | flops | bytes accessed | tf_op | source)
XLA Modules:
  0.0 367.9 jit_solution(2600039323009770919)
XLA Ops:
  7.2 0.8 slice_reduce_fusion.5
  8.1 1.8 fusion
  9.9 1.9 fusion.3
  12.3 1.0 fusion.56
  13.3 1.1 copy-done.3
  14.8 1.0 fusion.48
  15.8 1.0 copy-done.43
  16.8 2.6 multiply_convert_fusion.3
  19.4 2.6 multiply_convert_fusion.2
  22.0 1.0 fusion.50
  23.0 1.0 fusion.42
  24.0 3.2 pad_maximum_fusion.1
  28.6 65.2 %reduce-scatter.3.cloned.1.call-done = f32[1,512,768]{2,1,0:T(8,128)} async-done(((f32[4,512,768]{2,1,0:T(8,128)}), f32[1,512,768]{2,1,0:T(8,128)}) %reduce-scatter.3.cloned.1.call-update) | async-done | bytes 1572880 | tf_op jit(solution)/shard_map/reduce_scatter | solution.py:102
  93.8 1.6 fusion.122
  95.6 0.9 fusion.117
  96.9 0.7 multiply_reduce_fusion.7
  98.4 0.8 fusion.119
  99.8 0.7 multiply_reduce_fusion.9
  102.2 65.0 %all-gather.5.cloned.1.call-done = bf16[13,98304]{1,0:T(8,128)(2,1)} async-done(((bf16[13,768]{1,0:T(8,128)(2,1)}), bf16[13,98304]{1,0:T(8,128)(2,1)}) %all-gather.5.cloned.1.call-update) | async-done | bytes 2555920 | tf_op jit(solution)/shard_map/all_gather | solution.py:136
  167.2 2.7 slice.126
  169.9 3.3 reshape.167
  173.2 2.6 slice.127
  175.7 2.7 reshape.168
  178.4 2.7 slice_reduce_fusion.1
  181.6 1.0 copy.51
  182.7 2.7 fusion.123
  185.4 6.8 %select_reduce_fusion = f32[1024,16]{1,0:T(8,128)S(1)} fusion(f32[1024,512]{1,0:T(8,128)S(1)} %fusion.123, s32[1024,16]{1,0:T(8,128)S(1)} %copy-done.7), kind=kLoop, calls=%fused_computation | loop fusion | flops 25149440 | bytes 2228224 | tf_op jit(solution)/shard_map/reduce_sum | solution.py:156
  192.2 1.0 slice.128
  193.5 1.2 copy.56
  195.6 1.7 multiply_reduce_fusion.6
  197.9 2.4 fusion.28
  201.2 0.8 multiply_reduce_fusion.8
  202.1 1.0 fusion.31
  203.8 1.0 pad_maximum_fusion.2
  205.1 36.9 %all-gather.7.cloned.1.call-done = bf16[2048,768]{1,0:T(8,128)(2,1)} async-done(((bf16[512,768]{1,0:T(8,128)(2,1)}), bf16[2048,768]{1,0:T(8,128)(2,1)}) %all-gather.7.cloned.1.call-update) | async-done | bytes 3145744 | tf_op jit(solution)/shard_map/all_gather | solution.py:188
  242.0 2.2 fusion.121
  244.3 1.0 fusion.52
  245.5 1.0 convolution_bitcast_fusion.1
  246.5 1.0 fusion.44
  247.8 1.0 convolution_bitcast_fusion
  249.2 0.7 copy-done.50
  249.8 1.2 convolution_bitcast_fusion.3
  251.4 2.4 convolution_bitcast_fusion.5
  253.9 1.1 convolution_bitcast_fusion.2
  255.4 2.4 convolution_bitcast_fusion.4
  258.8 4.7 %pad_maximum_fusion = f32[768,3,2,512]{3,0,2,1:T(8,128)} fusion(f32[768,1,2,512]{3,0,2,1:T(8,128)S(1)} %maximum_bitcast_fusion.2, f32[768,1,2,512]{3,0,2,1:T(8,128)S(1)} %maximum_bitcast_fusion.1, f32[768,1,2,512]{3,0,2,1:T(8,128)S(1)} %maximum_bitcast_fusion), kind=kLoop, calls=%fused_computation.2 | loop fusion | flops 4718592 | bytes 18874368 | tf_op jit(solution)/shard_map/stack | solution.py:223
  263.5 96.1 %reduce-scatter.5.cloned.1.call-done = f32[24,3,2,512]{3,0,2,1:T(8,128)} async-done(((f32[768,3,2,512]{3,0,2,1:T(8,128)}), f32[24,3,2,512]{3,0,2,1:T(8,128)}) %reduce-scatter.5.cloned.1.call-update) | async-done | bytes 294928 | tf_op jit(solution)/shard_map/reduce_scatter | solution.py:225
  359.6 1.7 slice_bitcast_fusion
  (173 shorter events, 12.3 us)
Async XLA Ops:
  7.2 20.8 %copy-start = (s32[32,15]{0,1:T(8,128)S(1)}, s32[32,15]{0,1:T(8,128)}, u32[]{:S(2)}) copy-start(s32[32,15]{0,1:T(8,128)} %param.24) | copy-start | bytes 5764
  7.2 4.6 %copy-start.2 = (bf16[32,32,768]{2,1,0:T(8,128)(2,1)S(1)}, bf16[32,32,768]{2,1,0:T(8,128)(2,1)}, u32[]{:S(2)}) copy-start(bf16[32,32,768]{2,1,0:T(8,128)(2,1)} %param.13) | copy-start | bytes 4718596
  7.2 86.6 %reduce-scatter.3.cloned.1.call-start = ((), (), s32[]{:S(2)}) async-start(), calls=%async_computation.2 | async-start | bytes 7864320 | tf_op jit(solution)/shard_map/reduce_scatter | solution.py:102
  9.9 2.4 copy-start.42
  12.3 3.5 copy-start.12
  12.3 2.1 copy-start.3
  13.3 2.5 copy-start.49
  14.8 4.6 %copy-start.10 = (bf16[16,64,768]{2,1,0:T(8,128)(2,1)}, bf16[16,64,768]{2,1,0:T(8,128)(2,1)S(1)}, u32[]{:S(2)}) copy-start(bf16[16,64,768]{2,1,0:T(8,128)(2,1)S(1)} %fusion.5) | copy-start | bytes 4718596
  14.8 2.0 copy-start.43
  16.8 2.6 copy-start.47
  19.4 2.6 copy-start.16
  19.4 2.6 copy-start.8
  27.2 1.4 copy-start.30
  27.2 140.0 %all-gather.5.cloned.1.call-start = ((), (), s32[]{:S(2)}) async-start(), calls=%async_computation.4 | async-start | bytes 3170304 | tf_op jit(solution)/shard_map/all_gather | solution.py:136
  93.8 3.1 copy-start.40
  95.4 2.7 copy-start.4
  95.6 3.8 %copy-start.22 = (f32[8,32]{1,0:T(8,128)}, f32[8,32]{1,0:T(8,128)S(1)}, u32[]{:S(2)}) copy-start(f32[8,32]{1,0:T(8,128)S(1)} %multiply_reduce_fusion.5) | copy-start | bytes 3076
  97.6 2.9 copy-start.18
  97.7 3.0 copy-start.31
  98.3 2.2 copy-start.28
  99.2 70.7 %copy-start.35 = (f32[4]{0:T(128)}, f32[4]{0:T(128)S(1)}, u32[]{:S(2)}) copy-start(f32[4]{0:T(128)S(1)} %get-tuple-element.11) | copy-start | bytes 52
  100.5 72.6 %copy-start.20 = (f32[4,768]{1,0:T(4,128)}, f32[4,768]{1,0:T(4,128)S(1)}, u32[]{:S(2)}) copy-start(f32[4,768]{1,0:T(4,128)S(1)} %get-tuple-element.27) | copy-start | bytes 36868
  100.5 72.6 %copy-start.44 = (f32[4]{0:T(128)}, f32[4]{0:T(128)S(1)}, u32[]{:S(2)}) copy-start(f32[4]{0:T(128)S(1)} %get-tuple-element.26) | copy-start | bytes 52
  100.5 72.6 %copy-start.37 = (f32[4]{0:T(128)}, f32[4]{0:T(128)S(1)}, u32[]{:S(2)}) copy-start(f32[4]{0:T(128)S(1)} %add_rsqrt_fusion.2) | copy-start | bytes 52
  101.4 140.6 %all-gather.7.cloned.1.call-start = ((), (), s32[]{:S(2)}) async-start(), calls=%async_computation.5 | async-start | bytes 3932160 | tf_op jit(solution)/shard_map/all_gather | solution.py:188
  182.7 2.7 copy-start.7
  192.2 3.4 copy-start.19
  194.9 5.8 %copy-start.23 = (f32[8,32]{1,0:T(8,128)S(1)}, f32[8,32]{1,0:T(8,128)}, u32[]{:S(2)}) copy-start(f32[8,32]{1,0:T(8,128)} %copy-done.22) | copy-start | bytes 3076
  197.3 3.8 %copy-start.32 = (s32[4]{0:T(128)S(1)}, s32[4]{0:T(128)}, u32[]{:S(2)}) copy-start(s32[4]{0:T(128)} %multiply_add_fusion.2) | copy-start | bytes 52
  197.9 3.3 copy-start.6
  197.9 3.3 copy-start.21
  200.3 1.7 copy-start.45
  200.3 1.7 copy-start.36
  200.3 1.7 copy-start.38
  200.4 1.7 copy-start.41
  200.7 2.4 copy-start.5
  200.7 2.4 copy-start.25
  201.0 2.4 copy-start.29
  201.2 2.3 copy-start.27
  204.8 154.8 %reduce-scatter.5.cloned.1.call-start = ((), (), s32[]{:S(2)}) async-start(), calls=%async_computation.3 | async-start | bytes 9732096 | tf_op jit(solution)/shard_map/reduce_scatter | solution.py:225
  242.0 2.4 copy-start.9
  247.8 1.4 copy-start.13
  247.8 2.1 copy-start.50
  249.8 1.6 copy-start.52
  251.4 2.4 copy-start.11
  251.4 2.4 copy-start.48
  253.9 1.6 copy-start.51
  263.5 97.8 %copy-start.1 = (s32[32,15]{0,1:T(8,128)S(1)}, s32[32,15]{0,1:T(8,128)}, u32[]{:S(2)}) copy-start(s32[32,15]{0,1:T(8,128)} %param.24) | copy-start | bytes 5764
  (9 other events, 7.5 us)
Sparse Core Ops, SparseCore 0:
  27.3 66.4 reduce-scatter.2
  101.5 65.6 all-gather.4
  204.9 36.9 all-gather.6
  263.7 95.9 reduce-scatter.4

commit v8 on v7

--- a/solution.py
+++ b/solution.py
@@ -134,8 +134,10 @@
     packed = jnp.concatenate([query_round, passage_round, meta_flat], axis=0)
     devices = groups * segments
     gathered = lax.all_gather(packed[:, None, :], ("dp", "segment"), axis=1, tiled=True)
-    query_all = gathered[:query_dev].reshape(-1, model_width)
-    passage_all = gathered[query_dev : query_dev + passage_dev].reshape(-1, model_width)
+    query_all = gathered[:query_dev].reshape(query_dev, devices, model_width)
+    passage_all = gathered[query_dev : query_dev + passage_dev].reshape(
+        passage_dev, devices, model_width
+    )
     meta_all = (
         gathered[query_dev + passage_dev :]
         .transpose(1, 0, 2)
@@ -148,10 +150,10 @@
     cand_ids = meta_all[:, :slots] * id_radix + meta_all[:, slots : 2 * slots]
     cand_all = (cand_ids % passage_dev) * devices + cand_ids // passage_dev
     counts_all = meta_all[:, 2 * slots]
-    passage_total = passage_all.shape[0]
+    passage_total = passage_dev * devices
     all_scores = lax.dot_general(
-        query_all, passage_all, (((1,), (1,)), ((), ())), preferred_element_type=jnp.float32
-    )
+        query_all, passage_all, (((2,), (2,)), ((), ())), preferred_element_type=jnp.float32
+    ).reshape(query_dev * devices, passage_total)
     every_id = lax.broadcasted_iota(jnp.int32, (1, 1, passage_total), 2)
     scores = jnp.sum(
         jnp.where(cand_all[:, :, None] == every_id, all_scores[:, None, :], 0.0), axis=2
@@ -173,13 +175,17 @@
     passage_coef = jnp.sum(
         jnp.where(cand_all[:, :, None] == own_passages, score_grads[:, :, None], 0.0), axis=1
     )
-    query_grad = jnp.dot(
-        query_coef, passage_all.astype(jnp.float32), precision=lax.Precision.HIGHEST
+    query_grad = lax.dot_general(
+        query_coef.reshape(query_dev, passage_dev, devices),
+        passage_all.astype(jnp.float32),
+        (((1, 2), (0, 1)), ((), ())),
+        precision=lax.Precision.HIGHEST,
+        preferred_element_type=jnp.float32,
     )
     passage_grad = lax.dot_general(
-        passage_coef,
+        passage_coef.reshape(query_dev, devices, passage_dev),
         query_all.astype(jnp.float32),
-        (((0,), (0,)), ((), ())),
+        (((0, 1), (0, 1)), ((), ())),
         precision=lax.Precision.HIGHEST,
         preferred_element_type=jnp.float32,
     )

time: 369 us -> 368 us (level)
  local copies, waits for them, and re-layouts: 31.2 us -> 26.7 us
    reshape x2 -> x1, local copies, waits for them, and re-layouts: 5.99 us -> 0.15 us  [body(): passage_coef.reshape(query_dev, devices, passage_dev)]
    unnamed x113 -> x117, local copies, waits for them, and re-layouts: 7.67 us -> 10.1 us
where the time goes in v8:
time: 368 us; the launch traced here: 367 us
  waiting for transfers between devices  263 us (71%)
  matrix products  32 us (9%)
  other arithmetic  29.8 us (8%)
  local copies, waits for them, and re-layouts  26.7 us (7%)
  between operations  14.7 us (4%)
    reduce_scatter x1, waiting for transfers between devices, body(): lax.psum_scatter(weight_terms(), 'dp', scatter_dimension=0, tiled=True)  96.1 us
    reduce_scatter x1, waiting for transfers between devices, body(): lax.psum_scatter(jnp.concatenate([query_block, passage_block], axis=1), '...  65.2 us
    all_gather x1, waiting for transfers between devices, body(): lax.all_gather(packed[:, None, :], ('dp', 'segment'), axis=1, tiled=True)  65 us
    all_gather x1, waiting for transfers between devices, body(): lax.all_gather(jnp.concatenate([query_share.reshape(-1, model_width), pas...  36.9 us
    unnamed x117, local copies, waits for them, and re-layouts  10.1 us
    dot_general x6, matrix products, contract(): lax.dot_general(left, right, (((0,), (0,)), ((), ())), preferred_element_...  9.07 us
    reduce_sum x1, other arithmetic, body(): jnp.sum(jnp.where(cand_all[:, :, None] == every_id, all_scores[:, None, :...  8.12 us
  transfers between devices with their start and end apart: 4, of which 4 were waited for; matrix products, arithmetic and copies ran while one was open for 0% of the time, Pallas kernels for 0%

profile of v8, /device:TPU:0, one launch (start us, length us, event | category | flops | bytes accessed | tf_op | source)
XLA Modules:
  0.0 367.1 jit_solution(17799738843743577390)
XLA Ops:
  7.2 0.8 slice_reduce_fusion.5
  8.1 1.8 fusion
  9.9 1.9 fusion.3
  12.3 1.0 fusion.59
  13.3 1.1 copy-done.3
  14.8 1.0 fusion.51
  15.8 1.0 copy-done.44
  16.8 2.6 multiply_convert_fusion.3
  19.4 2.6 multiply_convert_fusion.2
  22.0 1.0 fusion.53
  23.0 1.0 fusion.45
  24.0 3.2 pad_maximum_fusion.1
  28.6 65.2 %reduce-scatter.3.cloned.1.call-done = f32[1,512,768]{2,1,0:T(8,128)} async-done(((f32[4,512,768]{2,1,0:T(8,128)}), f32[1,512,768]{2,1,0:T(8,128)}) %reduce-scatter.3.cloned.1.call-update) | async-done | bytes 1572880 | tf_op jit(solution)/shard_map/reduce_scatter | solution.py:102
  93.8 1.6 fusion.128
  95.6 0.9 fusion.123
  96.9 0.7 multiply_reduce_fusion.7
  98.3 0.8 fusion.125
  99.7 0.7 multiply_reduce_fusion.9
  102.1 65.0 %all-gather.5.cloned.1.call-done = bf16[13,98304]{1,0:T(8,128)(2,1)} async-done(((bf16[13,768]{1,0:T(8,128)(2,1)}), bf16[13,98304]{1,0:T(8,128)(2,1)}) %all-gather.5.cloned.1.call-update) | async-done | bytes 2555920 | tf_op jit(solution)/shard_map/all_gather | solution.py:136
  167.1 1.5 slice.126
  168.7 2.2 slice.127
  170.9 0.9 copy-done.7
  171.8 1.0 fusion.43
  173.4 1.5 copy.103
  174.9 2.7 slice_reduce_fusion.1
  178.2 1.0 copy.66
  179.1 8.1 %select_reduce_fusion = f32[1024,16]{1,0:T(8,128)S(1)} fusion(f32[1024,512]{1,0:T(8,128)} %bitcast.179, s32[1024,16]{1,0:T(8,128)} %copy.66), kind=kLoop, calls=%fused_computation | loop fusion | flops 25149440 | bytes 2228224 | tf_op jit(solution)/shard_map/reduce_sum | solution.py:158
  187.3 1.0 slice.128
  188.6 1.2 copy.82
  191.3 1.7 multiply_reduce_fusion.6
  193.0 2.3 fusion.28
  196.3 3.0 multiply_reduce_fusion.8
  200.0 2.3 fusion.31
  203.0 1.0 pad_maximum_fusion.2
  204.3 36.9 %all-gather.7.cloned.1.call-done = bf16[2048,768]{1,0:T(8,128)(2,1)} async-done(((bf16[512,768]{1,0:T(8,128)(2,1)}), bf16[2048,768]{1,0:T(8,128)(2,1)}) %all-gather.7.cloned.1.call-update) | async-done | bytes 3145744 | tf_op jit(solution)/shard_map/all_gather | solution.py:194
  241.2 2.2 fusion.127
  243.5 1.0 fusion.55
  244.7 1.0 convolution_bitcast_fusion.1
  245.8 1.0 fusion.47
  247.0 1.0 convolution_bitcast_fusion
  248.4 0.7 copy-done.51
  249.0 1.2 convolution_bitcast_fusion.3
  250.6 2.4 convolution_bitcast_fusion.5
  253.1 1.1 convolution_bitcast_fusion.2
  254.7 2.4 convolution_bitcast_fusion.4
  258.0 4.7 %pad_maximum_fusion = f32[768,3,2,512]{3,0,2,1:T(8,128)} fusion(f32[768,1,2,512]{3,0,2,1:T(8,128)S(1)} %maximum_bitcast_fusion.2, f32[768,1,2,512]{3,0,2,1:T(8,128)S(1)} %maximum_bitcast_fusion.1, f32[768,1,2,512]{3,0,2,1:T(8,128)S(1)} %maximum_bitcast_fusion), kind=kLoop, calls=%fused_computation.2 | loop fusion | flops 4718592 | bytes 18874368 | tf_op jit(solution)/shard_map/stack | solution.py:229
  262.7 96.1 %reduce-scatter.5.cloned.1.call-done = f32[24,3,2,512]{3,0,2,1:T(8,128)} async-done(((f32[768,3,2,512]{3,0,2,1:T(8,128)}), f32[24,3,2,512]{3,0,2,1:T(8,128)}) %reduce-scatter.5.cloned.1.call-update) | async-done | bytes 294928 | tf_op jit(solution)/shard_map/reduce_scatter | solution.py:231
  358.8 1.7 slice_bitcast_fusion
  (177 shorter events, 13.6 us)
Async XLA Ops:
  7.2 20.8 %copy-start = (s32[32,15]{0,1:T(8,128)S(1)}, s32[32,15]{0,1:T(8,128)}, u32[]{:S(2)}) copy-start(s32[32,15]{0,1:T(8,128)} %param.24) | copy-start | bytes 5764
  7.2 4.6 %copy-start.2 = (bf16[32,32,768]{2,1,0:T(8,128)(2,1)S(1)}, bf16[32,32,768]{2,1,0:T(8,128)(2,1)}, u32[]{:S(2)}) copy-start(bf16[32,32,768]{2,1,0:T(8,128)(2,1)} %param.13) | copy-start | bytes 4718596
  7.2 86.6 %reduce-scatter.3.cloned.1.call-start = ((), (), s32[]{:S(2)}) async-start(), calls=%async_computation.2 | async-start | bytes 7864320 | tf_op jit(solution)/shard_map/reduce_scatter | solution.py:102
  9.9 2.4 copy-start.43
  12.3 3.5 copy-start.12
  12.3 2.1 copy-start.3
  13.3 2.5 copy-start.50
  14.8 4.6 %copy-start.10 = (bf16[16,64,768]{2,1,0:T(8,128)(2,1)}, bf16[16,64,768]{2,1,0:T(8,128)(2,1)S(1)}, u32[]{:S(2)}) copy-start(bf16[16,64,768]{2,1,0:T(8,128)(2,1)S(1)} %fusion.5) | copy-start | bytes 4718596
  14.8 2.0 copy-start.44
  16.8 2.6 copy-start.48
  19.4 2.6 copy-start.16
  19.4 2.6 copy-start.8
  27.2 1.4 copy-start.32
  27.2 139.9 %all-gather.5.cloned.1.call-start = ((), (), s32[]{:S(2)}) async-start(), calls=%async_computation.4 | async-start | bytes 3170304 | tf_op jit(solution)/shard_map/all_gather | solution.py:136
  93.8 3.1 copy-start.42
  95.4 2.7 copy-start.4
  95.6 3.7 %copy-start.24 = (f32[8,32]{1,0:T(8,128)}, f32[8,32]{1,0:T(8,128)S(1)}, u32[]{:S(2)}) copy-start(f32[8,32]{1,0:T(8,128)S(1)} %multiply_reduce_fusion.5) | copy-start | bytes 3076
  97.6 2.9 copy-start.21
  97.7 2.9 copy-start.33
  98.3 2.2 copy-start.30
  99.1 69.5 %copy-start.38 = (f32[4]{0:T(128)}, f32[4]{0:T(128)S(1)}, u32[]{:S(2)}) copy-start(f32[4]{0:T(128)S(1)} %get-tuple-element.11) | copy-start | bytes 52
  100.5 70.4 %copy-start.23 = (f32[4,768]{1,0:T(4,128)}, f32[4,768]{1,0:T(4,128)S(1)}, u32[]{:S(2)}) copy-start(f32[4,768]{1,0:T(4,128)S(1)} %get-tuple-element.27) | copy-start | bytes 36868
  100.5 70.4 %copy-start.45 = (f32[4]{0:T(128)}, f32[4]{0:T(128)S(1)}, u32[]{:S(2)}) copy-start(f32[4]{0:T(128)S(1)} %get-tuple-element.26) | copy-start | bytes 52
  100.5 70.4 %copy-start.39 = (f32[4]{0:T(128)}, f32[4]{0:T(128)S(1)}, u32[]{:S(2)}) copy-start(f32[4]{0:T(128)S(1)} %add_rsqrt_fusion.2) | copy-start | bytes 52
  101.3 139.8 %all-gather.7.cloned.1.call-start = ((), (), s32[]{:S(2)}) async-start(), calls=%async_computation.5 | async-start | bytes 3932160 | tf_op jit(solution)/shard_map/all_gather | solution.py:194
  168.7 2.2 copy-start.6
  178.1 10.2 %copy-start.18 = (s32[1024,16]{0,1:T(8,128)}, s32[1024,16]{0,1:T(8,128)S(1)}, u32[]{:S(2)}) copy-start(s32[1024,16]{0,1:T(8,128)S(1)} %fusion.72) | copy-start | bytes 196612
  187.3 4.0 %copy-start.22 = (f32[8,768]{1,0:T(8,128)S(1)}, f32[8,768]{1,0:T(8,128)}, u32[]{:S(2)}) copy-start(f32[8,768]{1,0:T(8,128)} %copy-done.21) | copy-start | bytes 73732
  187.3 5.7 %copy-start.47 = (f32[8]{0:T(128)S(1)}, f32[8]{0:T(128)}, u32[]{:S(2)}) copy-start(f32[8]{0:T(128)} %copy-done.46) | copy-start | bytes 100
  187.3 5.7 %copy-start.34 = (f32[8]{0:T(128)S(1)}, f32[8]{0:T(128)}, u32[]{:S(2)}) copy-start(f32[8]{0:T(128)} %copy-done.33) | copy-start | bytes 100
  187.3 5.7 %copy-start.41 = (f32[8]{0:T(128)S(1)}, f32[8]{0:T(128)}, u32[]{:S(2)}) copy-start(f32[8]{0:T(128)} %copy-done.40) | copy-start | bytes 100
  190.0 5.7 %copy-start.25 = (f32[8,32]{1,0:T(8,128)S(1)}, f32[8,32]{1,0:T(8,128)}, u32[]{:S(2)}) copy-start(f32[8,32]{1,0:T(8,128)} %copy-done.24) | copy-start | bytes 3076
  192.9 3.0 copy-start.19
  192.9 3.0 copy-start.20
  193.0 3.0 copy-start.35
  196.0 6.3 %copy-start.5 = (bf16[16,64,768]{2,1,0:T(8,128)(2,1)S(1)}, bf16[16,64,768]{2,1,0:T(8,128)(2,1)}, u32[]{:S(2)}) copy-start(bf16[16,64,768]{2,1,0:T(8,128)(2,1)} %param.14) | copy-start | bytes 4718596
  196.0 6.3 %copy-start.27 = (f32[4,64]{1,0:T(4,128)S(1)}, f32[4,64]{1,0:T(4,128)}, u32[]{:S(2)}) copy-start(f32[4,64]{1,0:T(4,128)} %copy-done.26) | copy-start | bytes 3076
  196.3 6.3 %copy-start.31 = (f32[4,64]{1,0:T(4,128)S(1)}, f32[4,64]{1,0:T(4,128)}, u32[]{:S(2)}) copy-start(f32[4,64]{1,0:T(4,128)} %copy-done.30) | copy-start | bytes 3076
  196.3 6.4 %copy-start.29 = (f32[4,64]{1,0:T(4,128)S(1)}, f32[4,64]{1,0:T(4,128)}, u32[]{:S(2)}) copy-start(f32[4,64]{1,0:T(4,128)} %copy-done.28) | copy-start | bytes 3076
  204.0 154.8 %reduce-scatter.5.cloned.1.call-start = ((), (), s32[]{:S(2)}) async-start(), calls=%async_computation.3 | async-start | bytes 9732096 | tf_op jit(solution)/shard_map/reduce_scatter | solution.py:231
  241.2 2.4 copy-start.9
  247.0 1.4 copy-start.13
  247.0 2.1 copy-start.51
  249.0 1.6 copy-start.53
  250.6 2.4 copy-start.11
  250.6 2.4 copy-start.49
  253.1 1.6 copy-start.52
  262.7 97.8 %copy-start.1 = (s32[32,15]{0,1:T(8,128)S(1)}, s32[32,15]{0,1:T(8,128)}, u32[]{:S(2)}) copy-start(s32[32,15]{0,1:T(8,128)} %param.24) | copy-start | bytes 5764
  (10 other events, 8.4 us)
Sparse Core Ops, SparseCore 0:
  27.3 66.4 reduce-scatter.2
  101.4 65.6 all-gather.4
  204.1 36.9 all-gather.6
  262.9 95.9 reduce-scatter.4

commit v9 on v8

--- a/solution.py
+++ b/solution.py
@@ -155,25 +155,24 @@
         query_all, passage_all, (((2,), (2,)), ((), ())), preferred_element_type=jnp.float32
     ).reshape(query_dev * devices, passage_total)
     every_id = lax.broadcasted_iota(jnp.int32, (1, 1, passage_total), 2)
-    scores = jnp.sum(
-        jnp.where(cand_all[:, :, None] == every_id, all_scores[:, None, :], 0.0), axis=2
-    )
-    score_grads = score_grads_of(scores, counts_all)
     device_index = lax.axis_index("dp") * segments + segment_index
-    own_cand = lax.dynamic_index_in_dim(
-        cand_all.reshape(query_dev, devices, slots), device_index, 1, keepdims=False
-    )
-    own_grads = lax.dynamic_index_in_dim(
-        score_grads.reshape(query_dev, devices, slots), device_index, 1, keepdims=False
-    )
+    own_cand = (own_ids % passage_dev) * devices + own_ids // passage_dev
+    own_scores = jnp.sum(
+        jnp.where(
+            own_cand[:, :, None] == every_id,
+            lax.dot_general(
+                query_round,
+                passage_all,
+                (((1,), (2,)), ((), ())),
+                preferred_element_type=jnp.float32,
+            ).reshape(query_dev, 1, passage_total),
+            0.0,
+        ),
+        axis=2,
+    )
+    own_grads = score_grads_of(own_scores, own_rows(negative_counts, query_dev))
     query_coef = jnp.sum(
         jnp.where(own_cand[:, :, None] == every_id, own_grads[:, :, None], 0.0), axis=1
-    )
-    own_passages = (
-        lax.broadcasted_iota(jnp.int32, (1, 1, passage_dev), 2) * devices + device_index
-    )
-    passage_coef = jnp.sum(
-        jnp.where(cand_all[:, :, None] == own_passages, score_grads[:, :, None], 0.0), axis=1
     )
     query_grad = lax.dot_general(
         query_coef.reshape(query_dev, passage_dev, devices),
@@ -182,6 +181,18 @@
         precision=lax.Precision.HIGHEST,
         preferred_element_type=jnp.float32,
     )
+    query_share = query_back(query_grad)[0].astype(jnp.bfloat16)
+    query_rows = lax.all_gather(query_share, "segment", axis=0, tiled=True)
+    scores = jnp.sum(
+        jnp.where(cand_all[:, :, None] == every_id, all_scores[:, None, :], 0.0), axis=2
+    )
+    score_grads = score_grads_of(scores, counts_all)
+    own_passages = (
+        lax.broadcasted_iota(jnp.int32, (1, 1, passage_dev), 2) * devices + device_index
+    )
+    passage_coef = jnp.sum(
+        jnp.where(cand_all[:, :, None] == own_passages, score_grads[:, :, None], 0.0), axis=1
+    )
     passage_grad = lax.dot_general(
         passage_coef.reshape(query_dev, devices, passage_dev),
         query_all.astype(jnp.float32),
@@ -189,18 +200,8 @@
         precision=lax.Precision.HIGHEST,
         preferred_element_type=jnp.float32,
     )
-    query_share = query_back(query_grad)[0].astype(jnp.bfloat16)
     passage_share = passage_back(passage_grad)[0].astype(jnp.bfloat16)
-    share_rows = lax.all_gather(
-        jnp.concatenate(
-            [query_share.reshape(-1, model_width), passage_share.reshape(-1, model_width)], axis=0
-        ),
-        "segment",
-        axis=0,
-        tiled=False,
-    )
-    query_rows = share_rows[:, :query_size].reshape(query_states.shape)
-    passage_rows = share_rows[:, query_size:].reshape(passage_states.shape)
+    passage_rows = lax.all_gather(passage_share, "segment", axis=0, tiled=True)
 
     def backward_part(tower_parts, row_grads, tower_index):
         normed, up_pre, activated, gelu_back, hidden, branch = tower_parts

time: 368 us -> 377 us (1.024)
  matrix products: 32 us -> 38.5 us
  other arithmetic: 29.8 us -> 35 us
    dot_general x6, matrix products: 9.07 us -> 13.3 us  [contract(): lax.dot_general(left, right, (((0,), (0,)), ((), ())), preferred_element_...]
    all_gather x1 -> x2, waiting for transfers between devices: 36.9 us -> 39.1 us  [the longest x1 21.9 us: body(): query_rows = lax.all_gather(query_share, 'segment', axis=0, tiled=True)]
    unnamed x117 -> x136, local copies, waits for them, and re-layouts: 10.1 us -> 10.1 us
  transfers between devices with their start and end apart: 4 -> 5, of which waited for: 4 -> 5; matrix products, arithmetic and copies ran while one was open for 0% -> 4% of each run, Pallas kernels for 0% -> 0%
where the time goes in v9:
time: 377 us
  waiting for transfers between devices  264 us (70%)
  matrix products  38.5 us (10%)
  other arithmetic  35 us (9%)
  local copies, waits for them, and re-layouts  23.9 us (6%)
  between operations  14.7 us (4%)
    reduce_scatter x1, waiting for transfers between devices, body(): lax.psum_scatter(weight_terms(), 'dp', scatter_dimension=0, tiled=True)  95.9 us
    all_gather x1, waiting for transfers between devices, body(): lax.all_gather(packed[:, None, :], ('dp', 'segment'), axis=1, tiled=True)  65 us
    reduce_scatter x1, waiting for transfers between devices, body(): lax.psum_scatter(jnp.concatenate([query_block, passage_block], axis=1), '...  64 us
    all_gather x1, waiting for transfers between devices, body(): query_rows = lax.all_gather(query_share, 'segment', axis=0, tiled=True)  21.9 us
    all_gather x1, waiting for transfers between devices, body(): passage_rows = lax.all_gather(passage_share, 'segment', axis=0, tiled=True)  17.2 us
    dot_general x6, matrix products, contract(): lax.dot_general(left, right, (((0,), (0,)), ((), ())), preferred_element_...  13.3 us
    unnamed x136, local copies, waits for them, and re-layouts  10.1 us
    reduce_sum x1, other arithmetic, body(): jnp.sum(jnp.where(cand_all[:, :, None] == every_id, all_scores[:, None, :...  8.12 us
  transfers between devices with their start and end apart: 5, of which 5 were waited for; matrix products, arithmetic and copies ran while one was open for 4% of the time, Pallas kernels for 0%

profile of v9, /device:TPU:0, one launch (start us, length us, event | category | flops | bytes accessed | tf_op | source)
XLA Modules:
  0.0 376.8 jit_solution(3430648156366713207)
XLA Ops:
  7.2 0.8 slice_reduce_fusion.6
  8.1 1.8 fusion.3
  9.9 1.9 fusion
  12.3 1.0 fusion.52
  13.3 1.1 copy-done.3
  14.8 1.0 fusion.60
  15.8 1.0 copy-done.50
  16.8 2.6 multiply_convert_fusion.2
  19.4 2.6 multiply_convert_fusion.3
  22.0 1.0 fusion.46
  23.0 1.0 fusion.54
  24.0 3.2 pad_maximum_fusion.1
  29.7 64.0 %reduce-scatter.3.cloned.1.call-done = f32[1,512,768]{2,1,0:T(8,128)} async-done(((f32[4,512,768]{2,1,0:T(8,128)}), f32[1,512,768]{2,1,0:T(8,128)}) %reduce-scatter.3.cloned.1.call-update) | async-done | bytes 1572880 | tf_op jit(solution)/shard_map/reduce_scatter | solution.py:102
  93.7 1.6 fusion.144
  95.6 0.9 fusion.142
  98.6 0.8 fusion.140
  103.2 65.0 %all-gather.9.cloned.1.call-done = bf16[13,98304]{1,0:T(8,128)(2,1)} async-done(((bf16[13,768]{1,0:T(8,128)(2,1)}), bf16[13,98304]{1,0:T(8,128)(2,1)}) %all-gather.9.cloned.1.call-update) | async-done | bytes 2555920 | tf_op jit(solution)/shard_map/all_gather | solution.py:136
  168.2 2.7 slice_reduce_fusion.1
  171.5 1.8 slice.121
  173.3 1.0 convolution_bitcast_fusion.7
  174.4 1.1 copy-done.7
  175.6 1.0 fusion.42
  177.1 1.5 copy.103
  178.7 1.0 copy.65
  179.7 8.1 %select_reduce_fusion = f32[1024,16]{1,0:T(8,128)S(1)} fusion(f32[1024,512]{1,0:T(8,128)} %bitcast.173, s32[1024,16]{1,0:T(8,128)} %copy.65), kind=kLoop, calls=%fused_computation | loop fusion | flops 25149440 | bytes 2228224 | tf_op jit(solution)/shard_map/reduce_sum | solution.py:186
  188.7 1.6 fusion.138
  190.3 1.0 copy.69
  191.3 2.2 pad_add_fusion
  193.5 1.2 copy.70
  195.0 2.9 multiply_reduce_fusion.8
  198.0 2.3 fusion.31
  200.7 1.0 fusion.41
  202.9 1.7 multiply_reduce_fusion.6
  204.6 2.4 fusion.28
  207.4 1.0 fusion.40
  208.7 17.2 %all-gather.7.cloned.1.call-done = bf16[16,64,768]{2,1,0:T(8,128)(2,1)} async-done(((bf16[4,64,768]{2,1,0:T(8,128)(2,1)}), bf16[16,64,768]{2,1,0:T(8,128)(2,1)}) %all-gather.7.cloned.1.call-update) | async-done | bytes 1572880 | tf_op jit(solution)/shard_map/all_gather | solution.py:204
  225.9 3.7 convolution_bitcast_fusion
  229.6 2.3 fusion.48
  232.0 21.9 %all-gather.5.cloned.1.call-done = bf16[32,32,768]{2,1,0:T(8,128)(2,1)} async-done(((bf16[8,32,768]{2,1,0:T(8,128)(2,1)}), bf16[32,32,768]{2,1,0:T(8,128)(2,1)}) %all-gather.5.cloned.1.call-update) | async-done | bytes 1572880 | tf_op jit(solution)/shard_map/all_gather | solution.py:185
  253.9 2.6 convolution_bitcast_fusion.1
  256.5 1.0 fusion.56
  258.5 1.1 convolution_bitcast_fusion.2
  260.6 1.1 convolution_bitcast_fusion.3
  262.2 2.4 convolution_bitcast_fusion.4
  264.6 2.4 convolution_bitcast_fusion.5
  268.0 4.7 %pad_maximum_fusion = f32[768,3,2,512]{3,0,2,1:T(8,128)} fusion(f32[768,1,2,512]{3,0,2,1:T(8,128)S(1)} %maximum_bitcast_fusion.2, f32[768,1,2,512]{3,0,2,1:T(8,128)S(1)} %maximum_bitcast_fusion.1, f32[768,1,2,512]{3,0,2,1:T(8,128)S(1)} %maximum_bitcast_fusion), kind=kLoop, calls=%fused_computation.2 | loop fusion | flops 4718592 | bytes 18874368 | tf_op jit(solution)/shard_map/stack | solution.py:230
  272.7 95.9 %reduce-scatter.5.cloned.1.call-done = f32[24,3,2,512]{3,0,2,1:T(8,128)} async-done(((f32[768,3,2,512]{3,0,2,1:T(8,128)}), f32[24,3,2,512]{3,0,2,1:T(8,128)}) %reduce-scatter.5.cloned.1.call-update) | async-done | bytes 294928 | tf_op jit(solution)/shard_map/reduce_scatter | solution.py:232
  368.6 1.7 slice_bitcast_fusion
  (202 shorter events, 17.2 us)
Async XLA Ops:
  7.2 21.3 %copy-start = (s32[32,15]{0,1:T(8,128)S(1)}, s32[32,15]{0,1:T(8,128)}, u32[]{:S(2)}) copy-start(s32[32,15]{0,1:T(8,128)} %param.24) | copy-start | bytes 5764
  7.2 4.6 %copy-start.2 = (bf16[16,64,768]{2,1,0:T(8,128)(2,1)S(1)}, bf16[16,64,768]{2,1,0:T(8,128)(2,1)}, u32[]{:S(2)}) copy-start(bf16[16,64,768]{2,1,0:T(8,128)(2,1)} %param.14) | copy-start | bytes 4718596
  7.2 86.5 %reduce-scatter.3.cloned.1.call-start = ((), (), s32[]{:S(2)}) async-start(), calls=%async_computation.2 | async-start | bytes 7864320 | tf_op jit(solution)/shard_map/reduce_scatter | solution.py:102
  12.3 3.5 copy-start.13
  14.8 4.6 %copy-start.11 = (bf16[32,32,768]{2,1,0:T(8,128)(2,1)}, bf16[32,32,768]{2,1,0:T(8,128)(2,1)S(1)}, u32[]{:S(2)}) copy-start(bf16[32,32,768]{2,1,0:T(8,128)(2,1)S(1)} %fusion.2) | copy-start | bytes 4718596
  16.8 2.6 copy-start.59
  19.4 2.6 copy-start.18
  19.4 2.6 copy-start.9
  27.1 2.6 copy-start.36
  27.2 141.1 %all-gather.9.cloned.1.call-start = ((), (), s32[]{:S(2)}) async-start(), calls=%async_computation.6 | async-start | bytes 3170304 | tf_op jit(solution)/shard_map/all_gather | solution.py:136
  93.7 3.3 copy-start.48
  95.4 3.0 copy-start.4
  96.5 2.9 copy-start.43
  97.8 5.3 %copy-start.23 = (f32[4,768]{1,0:T(4,128)}, f32[4,768]{1,0:T(4,128)S(1)}, u32[]{:S(2)}) copy-start(f32[4,768]{1,0:T(4,128)S(1)} %get-tuple-element.30) | copy-start | bytes 36868
  97.9 5.3 %copy-start.45 = (f32[4]{0:T(128)}, f32[4]{0:T(128)S(1)}, u32[]{:S(2)}) copy-start(f32[4]{0:T(128)S(1)} %add_rsqrt_fusion.2) | copy-start | bytes 52
  98.6 4.6 %copy-start.27 = (f32[8,32]{1,0:T(8,128)}, f32[8,32]{1,0:T(8,128)S(1)}, u32[]{:S(2)}) copy-start(f32[8,32]{1,0:T(8,128)S(1)} %multiply_reduce_fusion.5) | copy-start | bytes 3076
  99.4 3.8 copy-start.41
  99.4 71.9 %copy-start.25 = (f32[8,32]{1,0:T(8,128)}, f32[8,32]{1,0:T(8,128)S(1)}, u32[]{:S(2)}) copy-start(f32[8,32]{1,0:T(8,128)S(1)} %get-tuple-element.38) | copy-start | bytes 3076
  100.5 2.7 copy-start.54
  100.5 2.7 copy-start.38
  102.4 123.5 %all-gather.7.cloned.1.call-start = ((), (), s32[]{:S(2)}) async-start(), calls=%async_computation.4 | async-start | bytes 1966080 | tf_op jit(solution)/shard_map/all_gather | solution.py:204
  171.3 3.0 copy-start.8
  188.0 6.7 %copy-start.40 = (s32[4]{0:T(128)S(1)}, s32[4]{0:T(128)}, u32[]{:S(2)}) copy-start(s32[4]{0:T(128)} %multiply_add_fusion.2) | copy-start | bytes 52
  188.7 6.3 %copy-start.24 = (f32[4,768]{1,0:T(4,128)S(1)}, f32[4,768]{1,0:T(4,128)}, u32[]{:S(2)}) copy-start(f32[4,768]{1,0:T(4,128)} %copy-done.23) | copy-start | bytes 36868
  191.3 6.6 %copy-start.57 = (f32[4]{0:T(128)S(1)}, f32[4]{0:T(128)}, u32[]{:S(2)}) copy-start(f32[4]{0:T(128)} %copy-done.56) | copy-start | bytes 52
  191.3 6.6 %copy-start.44 = (f32[4]{0:T(128)S(1)}, f32[4]{0:T(128)}, u32[]{:S(2)}) copy-start(f32[4]{0:T(128)} %copy-done.43) | copy-start | bytes 52
  191.3 6.6 %copy-start.46 = (f32[4]{0:T(128)S(1)}, f32[4]{0:T(128)}, u32[]{:S(2)}) copy-start(f32[4]{0:T(128)} %copy-done.45) | copy-start | bytes 52
  193.5 6.8 %copy-start.31 = (f32[4,64]{1,0:T(4,128)S(1)}, f32[4,64]{1,0:T(4,128)}, u32[]{:S(2)}) copy-start(f32[4,64]{1,0:T(4,128)} %copy-done.30) | copy-start | bytes 3076
  195.0 5.6 %copy-start.35 = (f32[4,64]{1,0:T(4,128)S(1)}, f32[4,64]{1,0:T(4,128)}, u32[]{:S(2)}) copy-start(f32[4,64]{1,0:T(4,128)} %copy-done.34) | copy-start | bytes 3076
  195.0 5.6 %copy-start.33 = (f32[4,64]{1,0:T(4,128)S(1)}, f32[4,64]{1,0:T(4,128)}, u32[]{:S(2)}) copy-start(f32[4,64]{1,0:T(4,128)} %copy-done.32) | copy-start | bytes 3076
  197.9 3.9 %copy-start.29 = (s32[8,16]{1,0:T(8,128)S(1)}, s32[8,16]{1,0:T(8,128)}, u32[]{:S(2)}) copy-start(s32[8,16]{1,0:T(8,128)} %get-tuple-element.22) | copy-start | bytes 1540
  198.0 4.1 %copy-start.37 = (s32[8]{0:T(128)S(1)}, s32[8]{0:T(128)}, u32[]{:S(2)}) copy-start(s32[8]{0:T(128)} %get-tuple-element.14) | copy-start | bytes 100
  198.0 4.9 %copy-start.22 = (f32[8,768]{1,0:T(8,128)S(1)}, f32[8,768]{1,0:T(8,128)}, u32[]{:S(2)}) copy-start(f32[8,768]{1,0:T(8,128)} %copy-done.21) | copy-start | bytes 73732
  200.3 4.2 %copy-start.55 = (f32[8]{0:T(128)S(1)}, f32[8]{0:T(128)}, u32[]{:S(2)}) copy-start(f32[8]{0:T(128)} %copy-done.54) | copy-start | bytes 100
  200.3 4.3 %copy-start.39 = (f32[8]{0:T(128)S(1)}, f32[8]{0:T(128)}, u32[]{:S(2)}) copy-start(f32[8]{0:T(128)} %copy-done.38) | copy-start | bytes 100
  200.3 4.2 %copy-start.42 = (f32[8]{0:T(128)S(1)}, f32[8]{0:T(128)}, u32[]{:S(2)}) copy-start(f32[8]{0:T(128)} %copy-done.41) | copy-start | bytes 100
  201.7 5.3 %copy-start.5 = (bf16[32,32,768]{2,1,0:T(8,128)(2,1)S(1)}, bf16[32,32,768]{2,1,0:T(8,128)(2,1)}, u32[]{:S(2)}) copy-start(bf16[32,32,768]{2,1,0:T(8,128)(2,1)} %param.13) | copy-start | bytes 4718596
  201.7 5.6 %copy-start.28 = (f32[8,32]{1,0:T(8,128)S(1)}, f32[8,32]{1,0:T(8,128)}, u32[]{:S(2)}) copy-start(f32[8,32]{1,0:T(8,128)} %copy-done.27) | copy-start | bytes 3076
  201.7 5.6 %copy-start.26 = (f32[8,32]{1,0:T(8,128)S(1)}, f32[8,32]{1,0:T(8,128)}, u32[]{:S(2)}) copy-start(f32[8,32]{1,0:T(8,128)} %copy-done.25) | copy-start | bytes 3076
  201.7 52.1 %all-gather.5.cloned.1.call-start = ((), (), s32[]{:S(2)}) async-start(), calls=%async_computation.3 | async-start | bytes 1966080 | tf_op jit(solution)/shard_map/all_gather | solution.py:185
  204.6 21.3 %copy-start.19 = (bf16[1024,512]{1,0:T(8,128)(2,1)S(1)}, bf16[1024,512]{1,0:T(8,128)(2,1)}, u32[]{:S(2)}) copy-start(bf16[1024,512]{1,0:T(8,128)(2,1)} %copy-done.18) | copy-start | bytes 3145732
  208.4 160.2 %reduce-scatter.5.cloned.1.call-start = ((), (), s32[]{:S(2)}) async-start(), calls=%async_computation.5 | async-start | bytes 9732096 | tf_op jit(solution)/shard_map/reduce_scatter | solution.py:232
  225.9 3.7 copy-start.10
  225.9 3.7 copy-start.51
  229.6 24.2 %copy-start.17 = (bf16[1024,512]{1,0:T(8,128)(2,1)S(1)}, bf16[1024,512]{1,0:T(8,128)(2,1)}, u32[]{:S(2)}) copy-start(bf16[1024,512]{1,0:T(8,128)(2,1)} %copy-done.16) | copy-start | bytes 3145732
  253.9 2.6 copy-start.52
  253.9 3.6 copy-start.62
  272.7 97.6 %copy-start.1 = (s32[32,15]{0,1:T(8,128)S(1)}, s32[32,15]{0,1:T(8,128)}, u32[]{:S(2)}) copy-start(s32[32,15]{0,1:T(8,128)} %param.24) | copy-start | bytes 5764
  (22 other events, 32.7 us)
Sparse Core Ops, SparseCore 0:
  27.3 66.4 reduce-scatter.2
  102.5 65.6 all-gather.8
  201.9 24.0 all-gather.6
  227.4 26.4 all-gather.4
  272.8 95.7 reduce-scatter.4

commit v10 on v8

--- a/solution.py
+++ b/solution.py
@@ -152,8 +152,11 @@
     counts_all = meta_all[:, 2 * slots]
     passage_total = passage_dev * devices
     all_scores = lax.dot_general(
-        query_all, passage_all, (((2,), (2,)), ((), ())), preferred_element_type=jnp.float32
-    ).reshape(query_dev * devices, passage_total)
+        gathered.reshape(-1, devices, model_width),
+        passage_all,
+        (((2,), (2,)), ((), ())),
+        preferred_element_type=jnp.float32,
+    )[:query_dev].reshape(query_dev * devices, passage_total)
     every_id = lax.broadcasted_iota(jnp.int32, (1, 1, passage_total), 2)
     scores = jnp.sum(
         jnp.where(cand_all[:, :, None] == every_id, all_scores[:, None, :], 0.0), axis=2
@@ -182,9 +185,13 @@
         precision=lax.Precision.HIGHEST,
         preferred_element_type=jnp.float32,
     )
+    slot_count = gathered.shape[0]
     passage_grad = lax.dot_general(
-        passage_coef.reshape(query_dev, devices, passage_dev),
-        query_all.astype(jnp.float32),
+        jnp.pad(
+            passage_coef.reshape(query_dev, devices, passage_dev),
+            ((0, slot_count - query_dev), (0, 0), (0, 0)),
+        ),
+        gathered.reshape(-1, devices, model_width).astype(jnp.float32),
         (((0, 1), (0, 1)), ((), ())),
         precision=lax.Precision.HIGHEST,
         preferred_element_type=jnp.float32,

time: 368 us -> 367 us (level)
    unnamed x117 -> x123, local copies, waits for them, and re-layouts: 10.1 us -> 13.9 us
where the time goes in v10:
time: 367 us; the launch traced here: 366 us
  waiting for transfers between devices  263 us (72%)
  local copies, waits for them, and re-layouts  30.1 us (8%)
  matrix products  29.6 us (8%)
  other arithmetic  27.8 us (8%)
  between operations  14.7 us (4%)
    reduce_scatter x1, waiting for transfers between devices, body(): lax.psum_scatter(weight_terms(), 'dp', scatter_dimension=0, tiled=True)  96.1 us
    reduce_scatter x1, waiting for transfers between devices, body(): lax.psum_scatter(jnp.concatenate([query_block, passage_block], axis=1), '...  65.3 us
    all_gather x1, waiting for transfers between devices, body(): lax.all_gather(packed[:, None, :], ('dp', 'segment'), axis=1, tiled=True)  65 us
    all_gather x1, waiting for transfers between devices, body(): lax.all_gather(jnp.concatenate([query_share.reshape(-1, model_width), pas...  36.9 us
    unnamed x123, local copies, waits for them, and re-layouts  13.9 us
    dot_general x6, matrix products, contract(): lax.dot_general(left, right, (((0,), (0,)), ((), ())), preferred_element_...  9.08 us
  transfers between devices with their start and end apart: 4, of which 4 were waited for; matrix products, arithmetic and copies ran while one was open for 0% of the time, Pallas kernels for 0%

profile of v10, /device:TPU:0, one launch (start us, length us, event | category | flops | bytes accessed | tf_op | source)
XLA Modules:
  0.0 366.1 jit_solution(11758631749253842406)
XLA Ops:
  7.2 1.9 fusion.3
  9.1 0.8 slice_reduce_fusion.5
  11.8 1.2 copy-done.45
  13.0 1.0 fusion.57
  14.0 1.0 fusion.65
  14.9 1.2 copy-done.46
  16.1 2.6 multiply_convert_fusion.3
  18.8 2.6 multiply_convert_fusion.2
  21.4 1.0 fusion.59
  22.4 1.0 fusion.51
  23.4 3.2 pad_maximum_fusion.1
  28.0 65.3 %reduce-scatter.3.cloned.1.call-done = f32[1,512,768]{2,1,0:T(8,128)} async-done(((f32[4,512,768]{2,1,0:T(8,128)}), f32[1,512,768]{2,1,0:T(8,128)}) %reduce-scatter.3.cloned.1.call-update) | async-done | bytes 1572880 | tf_op jit(solution)/shard_map/reduce_scatter | solution.py:102
  93.2 1.5 fusion.135
  94.7 1.3 multiply_reduce_fusion.5
  96.3 0.8 fusion.132
  97.7 0.7 multiply_reduce_fusion.9
  99.0 0.8 fusion.130
  99.8 1.3 multiply_reduce_fusion.4
  101.1 0.7 multiply_reduce_fusion.7
  104.0 65.0 %all-gather.5.cloned.1.call-done = bf16[13,98304]{1,0:T(8,128)(2,1)} async-done(((bf16[13,768]{1,0:T(8,128)(2,1)}), bf16[13,98304]{1,0:T(8,128)(2,1)}) %all-gather.5.cloned.1.call-update) | async-done | bytes 2555920 | tf_op jit(solution)/shard_map/all_gather | solution.py:136
  169.0 2.7 slice_reduce_fusion.1
  172.3 1.0 copy.60
  173.3 2.6 copy.74
  175.9 2.7 slice.125
  178.7 0.9 copy-done.6
  179.6 1.0 fusion.6
  180.6 1.4 copy.67
  182.2 0.9 copy-done.8
  183.0 6.8 %select_reduce_fusion = f32[1024,16]{1,0:T(8,128)S(1)} fusion(f32[1024,512]{1,0:T(8,128)S(1)} %bitcast.185, s32[1024,16]{1,0:T(8,128)S(1)} %copy-done.8), kind=kLoop, calls=%fused_computation | loop fusion | flops 25149440 | bytes 2228224 | tf_op jit(solution)/shard_map/reduce_sum | solution.py:161
  190.1 1.0 slice.126
  191.1 1.2 copy.71
  192.9 2.9 multiply_reduce_fusion.8
  196.2 2.4 fusion.35
  200.3 1.0 fusion.32
  202.0 1.0 pad_maximum_fusion.2
  203.2 36.9 %all-gather.7.cloned.1.call-done = bf16[2048,768]{1,0:T(8,128)(2,1)} async-done(((bf16[512,768]{1,0:T(8,128)(2,1)}), bf16[2048,768]{1,0:T(8,128)(2,1)}) %all-gather.7.cloned.1.call-update) | async-done | bytes 3145744 | tf_op jit(solution)/shard_map/all_gather | solution.py:201
  240.1 2.2 fusion.134
  242.3 1.0 convolution_bitcast_fusion
  243.7 1.0 fusion.53
  245.0 1.0 convolution_bitcast_fusion.1
  246.0 1.0 fusion.61
  248.0 1.2 convolution_bitcast_fusion.2
  249.6 2.4 convolution_bitcast_fusion.4
  252.1 1.1 convolution_bitcast_fusion.3
  253.7 2.4 convolution_bitcast_fusion.5
  257.0 4.7 %pad_maximum_fusion = f32[768,3,2,512]{3,0,2,1:T(8,128)} fusion(f32[768,1,2,512]{3,0,2,1:T(8,128)S(1)} %maximum_bitcast_fusion.2, f32[768,1,2,512]{3,0,2,1:T(8,128)S(1)} %maximum_bitcast_fusion.1, f32[768,1,2,512]{3,0,2,1:T(8,128)S(1)} %maximum_bitcast_fusion), kind=kLoop, calls=%fused_computation.2 | loop fusion | flops 4718592 | bytes 18874368 | tf_op jit(solution)/shard_map/stack | solution.py:236
  261.8 96.1 %reduce-scatter.5.cloned.1.call-done = f32[24,3,2,512]{3,0,2,1:T(8,128)} async-done(((f32[768,3,2,512]{3,0,2,1:T(8,128)}), f32[24,3,2,512]{3,0,2,1:T(8,128)}) %reduce-scatter.5.cloned.1.call-update) | async-done | bytes 294928 | tf_op jit(solution)/shard_map/reduce_scatter | solution.py:238
  357.8 1.7 slice_bitcast_fusion
  (181 shorter events, 14.3 us)
Async XLA Ops:
  7.2 20.3 %copy-start = (s32[32,15]{0,1:T(8,128)S(1)}, s32[32,15]{0,1:T(8,128)}, u32[]{:S(2)}) copy-start(s32[32,15]{0,1:T(8,128)} %param.24) | copy-start | bytes 5764
  7.2 2.8 copy-start.3
  7.2 86.0 %reduce-scatter.3.cloned.1.call-start = ((), (), s32[]{:S(2)}) async-start(), calls=%async_computation.2 | async-start | bytes 7864320 | tf_op jit(solution)/shard_map/reduce_scatter | solution.py:102
  9.9 1.4 copy-start.2
  10.8 4.1 %copy-start.11 = (bf16[32,32,768]{2,1,0:T(8,128)(2,1)}, bf16[32,32,768]{2,1,0:T(8,128)(2,1)S(1)}, u32[]{:S(2)}) copy-start(bf16[32,32,768]{2,1,0:T(8,128)(2,1)S(1)} %fusion.2) | copy-start | bytes 4718596
  10.8 2.2 copy-start.45
  11.8 6.9 %copy-start.13 = (bf16[16,64,768]{2,1,0:T(8,128)(2,1)}, bf16[16,64,768]{2,1,0:T(8,128)(2,1)S(1)}, u32[]{:S(2)}) copy-start(bf16[16,64,768]{2,1,0:T(8,128)(2,1)S(1)} %fusion.5) | copy-start | bytes 4718596
  13.9 4.8 %copy-start.53 = (f32[1024,512]{1,0:T(8,128)}, f32[1024,512]{1,0:T(8,128)S(1)}, u32[]{:S(2)}) copy-start(f32[1024,512]{1,0:T(8,128)S(1)} %fusion.57) | copy-start | bytes 6291460
  13.9 2.2 copy-start.46
  16.1 2.6 copy-start.51
  18.7 2.6 copy-start.15
  18.7 2.6 copy-start.9
  26.6 142.4 %all-gather.5.cloned.1.call-start = ((), (), s32[]{:S(2)}) async-start(), calls=%async_computation.4 | async-start | bytes 3170304 | tf_op jit(solution)/shard_map/all_gather | solution.py:136
  94.7 3.0 copy-start.43
  96.0 5.1 %copy-start.23 = (f32[8,32]{1,0:T(8,128)}, f32[8,32]{1,0:T(8,128)S(1)}, u32[]{:S(2)}) copy-start(f32[8,32]{1,0:T(8,128)S(1)} %multiply_reduce_fusion.5) | copy-start | bytes 3076
  97.1 2.7 copy-start.39
  98.4 5.6 %copy-start.21 = (f32[4,768]{1,0:T(4,128)}, f32[4,768]{1,0:T(4,128)S(1)}, u32[]{:S(2)}) copy-start(f32[4,768]{1,0:T(4,128)S(1)} %get-tuple-element.27) | copy-start | bytes 36868
  99.0 5.0 %copy-start.41 = (f32[4]{0:T(128)}, f32[4]{0:T(128)S(1)}, u32[]{:S(2)}) copy-start(f32[4]{0:T(128)S(1)} %add_rsqrt_fusion.2) | copy-start | bytes 52
  99.8 4.2 %copy-start.37 = (f32[8]{0:T(128)}, f32[8]{0:T(128)S(1)}, u32[]{:S(2)}) copy-start(f32[8]{0:T(128)S(1)} %get-tuple-element.9) | copy-start | bytes 100
  101.9 2.1 copy-start.32
  103.2 136.9 %all-gather.7.cloned.1.call-start = ((), (), s32[]{:S(2)}) async-start(), calls=%async_computation.5 | async-start | bytes 3932160 | tf_op jit(solution)/shard_map/all_gather | solution.py:201
  175.9 4.7 %copy-start.5 = (bf16[2,8,128,768]{3,2,1,0:T(8,128)(2,1)}, bf16[2,8,128,768]{3,2,1,0:T(8,128)(2,1)S(1)}, u32[]{:S(2)}) copy-start(bf16[2,8,128,768]{3,2,1,0:T(8,128)(2,1)S(1)} %copy.74) | copy-start | bytes 9437188
  189.9 2.9 copy-start.34
  189.9 3.0 copy-start.22
  191.1 4.8 %copy-start.50 = (f32[4]{0:T(128)S(1)}, f32[4]{0:T(128)}, u32[]{:S(2)}) copy-start(f32[4]{0:T(128)} %copy-done.49) | copy-start | bytes 52
  192.3 3.8 %copy-start.40 = (f32[4]{0:T(128)S(1)}, f32[4]{0:T(128)}, u32[]{:S(2)}) copy-start(f32[4]{0:T(128)} %copy-done.39) | copy-start | bytes 52
  192.3 3.8 %copy-start.42 = (f32[4]{0:T(128)S(1)}, f32[4]{0:T(128)}, u32[]{:S(2)}) copy-start(f32[4]{0:T(128)} %copy-done.41) | copy-start | bytes 52
  192.9 5.6 %copy-start.26 = (f32[4,64]{1,0:T(4,128)S(1)}, f32[4,64]{1,0:T(4,128)}, u32[]{:S(2)}) copy-start(f32[4,64]{1,0:T(4,128)} %copy-done.25) | copy-start | bytes 3076
  192.9 6.0 %copy-start.30 = (f32[4,64]{1,0:T(4,128)S(1)}, f32[4,64]{1,0:T(4,128)}, u32[]{:S(2)}) copy-start(f32[4,64]{1,0:T(4,128)} %copy-done.29) | copy-start | bytes 3076
  192.9 6.0 %copy-start.28 = (f32[4,64]{1,0:T(4,128)S(1)}, f32[4,64]{1,0:T(4,128)}, u32[]{:S(2)}) copy-start(f32[4,64]{1,0:T(4,128)} %copy-done.27) | copy-start | bytes 3076
  196.0 3.4 copy-start.20
  196.2 3.3 copy-start.7
  198.6 1.4 copy-start.48
  198.6 1.4 copy-start.33
  198.6 1.4 copy-start.38
  198.6 1.7 copy-start.44
  198.9 2.4 copy-start.4
  199.2 2.4 copy-start.24
  203.0 154.9 %reduce-scatter.5.cloned.1.call-start = ((), (), s32[]{:S(2)}) async-start(), calls=%async_computation.3 | async-start | bytes 9732096 | tf_op jit(solution)/shard_map/reduce_scatter | solution.py:238
  240.1 2.2 copy-start.18
  242.3 1.4 copy-start.10
  246.0 1.4 copy-start.14
  246.0 2.1 copy-start.54
  248.0 1.6 copy-start.56
  249.6 2.4 copy-start.12
  249.6 2.4 copy-start.52
  252.1 1.6 copy-start.55
  261.7 97.8 %copy-start.1 = (s32[32,15]{0,1:T(8,128)S(1)}, s32[32,15]{0,1:T(8,128)}, u32[]{:S(2)}) copy-start(s32[32,15]{0,1:T(8,128)} %param.24) | copy-start | bytes 5764
  (13 other events, 11.6 us)
Sparse Core Ops, SparseCore 0:
  26.7 66.4 reduce-scatter.2
  103.3 65.6 all-gather.4
  203.1 36.9 all-gather.6
  261.9 95.9 reduce-scatter.4
